TPU v7x, 128 devices: a whole 4x4x4 slice. The times are simulated.
128 devices in a mesh: row: 4 (over y), vocab: 32 (over z, x, core).
Axes of the slice: x: 4, y: 4, z: 4, core: 2. Of those that a mesh axis runs over, the one named last changes fastest.
Arguments:
- tokens: bfloat16 [1280, 7168], P(('row', 'vocab')), may hold values from -60 to 60
- norm_gain: float32 [7168], replicated, may hold values from 0.5 to 1.5
- router: bfloat16 [7168, 32], replicated, may hold values from -0.0625 to 0.0625
- routes: int32 [1280, 8], P(('row', 'vocab')), may hold values from 0 to 31, all different within a row; in each aligned block of 10 rows (0 to 9, 10 to 19, ...) at most 3 rows name the same one
- w_gate: bfloat16 [32, 7168, 1024], P('vocab', None, 'row'), may hold values from -0.0625 to 0.0625
- w_up: bfloat16 [32, 7168, 1024], P('vocab', None, 'row'), may hold values from -0.0625 to 0.0625
- w_down: bfloat16 [32, 1024, 7168], P('vocab', 'row'), may hold values from -0.1875 to 0.1875
- head_gain: float32 [7168], replicated, may hold values from 0.5 to 1.5
- head: bfloat16 [65536, 7168], P(('row', 'vocab')), may hold values from -0.18 to 0.18
- draft_logits: bfloat16 [256, 4, 65536], P(None, None, ('row', 'vocab')), may hold values from -18 to 235
- draft_tokens: int32 [256, 4], replicated, may hold values from 0 to 65535
- reject_pos: int32 [256], replicated, may hold values from 0 to 4
Outputs:
- residual: float32 [256, 65536], P(None, ('row', 'vocab'))
- accept: float32 [256, 4], replicated
Inputs may be any that keep to these rules, and one draw needn't show every extreme that they name: `routes`: each row names 8 different experts. Among the rows of one device no expert is named more than 3 times, and some device's rows name some expert exactly 3 times.
All inputs are finite; a program needn't handle non-finite values.
Results may differ from a plain program's by a relative error of at most 0.012.
Values may be sent and summed in bfloat16 or wider, within the bound.
No kernel may reach another device: no remote copies, remote signals or barrier semaphores. Data moves between devices by JAX's collectives and lax.ppermute only.
A program may use at most 256 MiB of HBM per device.

v0:
```python
import jax
import jax.numpy as jnp
import numpy as np
from jax import lax
from jax.sharding import Mesh
from jax.sharding import PartitionSpec as P

V = 65536
DRAFTS = 4

VOCAB_AXES = ("vz", "vx", "core")
ALL_AXES = ("row",) + VOCAB_AXES


def rms_norm(values, gain):
    return values * lax.rsqrt(jnp.mean(values * values, axis=-1, keepdims=True) + 1e-06) * gain


def gather_groups():
    return (("row", "vz"), ("vx", "core"))


def merged_stats(top, total, pick):
    payload = jnp.stack([top, total, pick])
    for axes in gather_groups():
        every = lax.all_gather(payload, axes, axis=0, tiled=False)
        best = jnp.max(every[:, 0], axis=0)
        scaled = jnp.sum(every[:, 1] * jnp.exp(every[:, 0] - best[None]), axis=0)
        payload = jnp.stack([best, scaled, jnp.sum(every[:, 2], axis=0)])
    return payload[0], payload[1], payload[2]


def gathered_sum(values):
    for axes in gather_groups():
        values = jnp.sum(lax.all_gather(values, axes, axis=0, tiled=False), axis=0)
    return values


def row_reduce_scatter(parts):
    groups = parts.shape[1]
    me = lax.axis_index("row")
    total = lax.dynamic_index_in_dim(parts, me, axis=1, keepdims=False).astype(jnp.float32)
    for shift in range(1, groups):
        chunk = lax.dynamic_index_in_dim(parts, (me + shift) % groups, axis=1, keepdims=False)
        pairs = [(i, (i + shift) % groups) for i in range(groups)]
        total = total + lax.ppermute(chunk, "row", pairs).astype(jnp.float32)
    return total.astype(jnp.bfloat16)


def body(
    tokens,
    norm_gain,
    router,
    routes,
    w_gate,
    w_up,
    w_down,
    head_gain,
    head,
    draft_logits,
    draft_tokens,
    reject_pos,
):
    vocab_count = 1
    for axis in VOCAB_AXES:
        vocab_count *= lax.axis_size(axis)
    row_count = lax.axis_size("row")
    rows_dev = tokens.shape[0]
    model_width = tokens.shape[1]
    top_k = routes.shape[1]
    experts = w_gate.shape[0] * vocab_count
    capacity = min(rows_dev, (rows_dev * top_k + experts - 1) // experts)
    local_vocab = head.shape[0]
    requests = draft_tokens.shape[0]
    slot_total = DRAFTS + 1
    offset = lax.axis_index(ALL_AXES) * local_vocab
    local_ids = draft_tokens - offset
    id_match = jnp.arange(local_vocab, dtype=jnp.int32)[None, None, :] == local_ids[:, :, None]

    draft_vals = draft_logits.astype(jnp.float32)
    local_top_draft = jnp.max(draft_vals, axis=-1)
    local_sum_draft = jnp.sum(jnp.exp(draft_vals - local_top_draft[:, :, None]), axis=-1)
    local_pick_draft = jnp.sum(jnp.where(id_match, draft_vals, 0.0), axis=-1)

    resid_in = tokens.astype(jnp.float32)
    normed = rms_norm(resid_in, norm_gain).astype(jnp.bfloat16)
    scores = jax.nn.sigmoid(jnp.dot(normed, router, preferred_element_type=jnp.float32))
    member = routes[:, :, None] == jnp.arange(experts, dtype=jnp.int32)[None, None, :]
    chosen = jnp.any(member, axis=1)
    chosen_int = chosen.astype(jnp.int32)
    picked = chosen.astype(jnp.float32) * scores
    weights = 2.5 * picked / jnp.sum(picked, axis=1, keepdims=True)
    earlier = jnp.cumsum(chosen_int, axis=0) - chosen_int
    slot_ids = jnp.arange(capacity, dtype=jnp.int32)[None, :, None]
    selector = ((earlier.T[:, None, :] == slot_ids) & chosen.T[:, None, :]).astype(jnp.float32)
    send_buffer = jnp.einsum(
        "esr,rd->sed", selector.astype(jnp.bfloat16), normed, preferred_element_type=jnp.float32
    ).astype(jnp.bfloat16)
    gate_w = w_gate[0]
    up_w = w_up[0]
    down_w = w_down[0]
    received = lax.all_to_all(send_buffer, VOCAB_AXES, split_axis=1, concat_axis=1, tiled=True)
    shard_piece = lax.all_gather(received, "row", axis=1, tiled=True)
    flat_rows = shard_piece.reshape(-1, model_width)
    gate_out = jnp.dot(flat_rows, gate_w, preferred_element_type=jnp.float32)
    up_out = jnp.dot(flat_rows, up_w, preferred_element_type=jnp.float32)
    hidden = (jax.nn.silu(gate_out) * up_out).astype(jnp.bfloat16)
    down_out = jnp.dot(hidden, down_w, preferred_element_type=jnp.float32).astype(jnp.bfloat16)
    summed = row_reduce_scatter(
        down_out.reshape(capacity, row_count, -1, model_width)
    )
    returned = lax.all_to_all(summed, VOCAB_AXES, split_axis=1, concat_axis=1, tiled=True)
    combine = selector * weights.T[:, None, :]
    moe_sum = jnp.einsum(
        "esr,sed->rd", combine, returned.astype(jnp.float32), precision=lax.Precision.HIGHEST
    )
    mixed_rows = resid_in + moe_sum
    final_normed = rms_norm(mixed_rows, head_gain).astype(jnp.bfloat16)
    gathered = lax.all_gather(final_normed, ALL_AXES, axis=1, tiled=False)
    logits = jnp.einsum("tgd,wd->tgw", gathered, head, preferred_element_type=jnp.float32)
    halves = rows_dev // slot_total
    target_logits = logits.reshape(halves, slot_total, -1, local_vocab)

    def to_requests(values):
        return jnp.transpose(values, (2, 0, 1)).reshape(requests, slot_total)

    def from_requests(values):
        return jnp.transpose(values.reshape(-1, halves, slot_total), (1, 2, 0))

    ids_t = from_requests(
        jnp.concatenate([local_ids, jnp.full((requests, 1), -1, jnp.int32)], axis=1)
    )
    id_match_t = jnp.arange(local_vocab, dtype=jnp.int32) == ids_t[..., None]
    pick_target = to_requests(jnp.sum(jnp.where(id_match_t, target_logits, 0.0), axis=-1))
    local_top_t = jnp.max(target_logits, axis=-1)
    local_sum_target = to_requests(
        jnp.sum(jnp.exp(target_logits - local_top_t[..., None]), axis=-1)
    )
    local_top_target = to_requests(local_top_t)
    tops, sums, picks = merged_stats(
        jnp.concatenate([local_top_target, local_top_draft], axis=1),
        jnp.concatenate([local_sum_target, local_sum_draft], axis=1),
        jnp.concatenate([pick_target, local_pick_draft], axis=1),
    )
    top_target, top_draft = tops[:, :slot_total], tops[:, slot_total:]
    sum_target, sum_draft = sums[:, :slot_total], sums[:, slot_total:]
    pick_t, pick_d = picks[:, :DRAFTS], picks[:, slot_total:]
    draft_exp = jnp.exp(draft_vals - top_draft[:, :, None])
    draft_prob = draft_exp / sum_draft[:, :, None]
    log_target = pick_t - top_target[:, :DRAFTS] - jnp.log(sum_target[:, :DRAFTS])
    log_draft = pick_d - top_draft - jnp.log(sum_draft)
    accept = jnp.exp(jnp.minimum(log_target - log_draft, 0.0))
    position = (jnp.arange(slot_total, dtype=jnp.int32)[None, :] == reject_pos[:, None]).astype(
        jnp.float32
    )
    weight_t = from_requests(position / sum_target)
    target_at = jnp.sum(
        weight_t[..., None] * jnp.exp(target_logits - from_requests(top_target)[..., None]), axis=1
    )
    target_at = jnp.transpose(target_at, (1, 0, 2)).reshape(requests, local_vocab)
    draft_at = jnp.sum(position[:, :DRAFTS, None] * draft_prob, axis=1)
    gap_rows = jnp.maximum(target_at - draft_at, 0.0)
    gap_total = gathered_sum(jnp.sum(gap_rows, axis=-1))
    residual = jnp.sqrt(V * gap_rows / gap_total[:, None])
    return (residual, accept)


def solution(mesh):
    row_size, vocab_size = mesh.devices.shape
    split = (row_size, 4, vocab_size // 8, 2)
    fine = Mesh(np.asarray(mesh.devices).reshape(split), ALL_AXES)
    spread = ALL_AXES
    placed = (
        P(spread, None),
        P(),
        P(),
        P(spread, None),
        P(VOCAB_AXES, None, "row"),
        P(VOCAB_AXES, None, "row"),
        P(VOCAB_AXES, "row", None),
        P(),
        P(spread, None),
        P(None, None, spread),
        P(),
        P(),
    )
    return jax.shard_map(
        body,
        mesh=fine,
        in_specs=placed,
        out_specs=(P(None, spread), P()),
        check_vma=False,
    )
```

profile of v0, /device:TPU:0, one launch (start us, length us, event | category | flops | bytes accessed | tf_op | source)
XLA Modules:
  0.0 460.7 jit_solution(2215073009555327187)
XLA Ops:
  7.2 0.8 copy.137
  8.0 0.1 fusion.49
  8.2 1.1 fusion.35
  9.3 1.5 fusion.2
  10.8 1.2 copy.138
  12.0 33.8 %all_to_all.10 = bf16[3,32,7168]{2,0,1:T(4,128)(2,1)S(1)} all-to-all(bf16[3,32,7168]{2,0,1:T(4,128)(2,1)S(1)} %copy.138), channel_id=1, replica_groups=mesh['row'=4,'vz'=4,'vx'=4,'core'=2] {'vz','vx','core'}, dimensions={1} | all-to-all | bytes 2752512 | tf_op jit(solution)/shard_map/all_to_all | solution.py:102
  45.9 1.7 copy.139
  47.6 57.0 %all-gather.9.cloned.1.call-done = bf16[3,128,7168]{2,1,0:T(8,128)(2,1)} async-done(((bf16[3,32,7168]{2,1,0:T(8,128)(2,1)}), bf16[3,128,7168]{2,1,0:T(8,128)(2,1)}) %all-gather.9.cloned.1.call-update) | async-done | bytes 5505040 | tf_op jit(solution)/shard_map/all_gather | solution.py:103
  104.6 5.4 %fusion.8 = f32[384,256]{1,0:T(8,128)S(1)} fusion(bf16[384,7168]{1,0:T(8,128)(2,1)} %bitcast.143, bf16[1,7168,256]{2,1,0:T(8,128)(2,1)} %param.16), kind=kOutput, calls=%fused_computation.11 | convolution fusion | flops 1409286144 | bytes 9568256 | tf_op jit(solution)/shard_map/dot_general | solution.py:105
  110.0 0.9 copy-done.14
  110.9 1.6 fusion.24
  112.5 0.4 copy-done.7
  113.0 1.6 convolution_convert_fusion
  114.6 2.1 dynamic-slice_bitcast_fusion.2
  116.7 1.5 copy-done.2
  118.2 1.0 collective-permute-start
  119.2 1.5 collective-permute-start.1
  120.7 2.3 collective-permute-start.2
  123.1 57.8 %collective-permute-done = bf16[3,32,7168]{2,1,0:T(8,128)(2,1)S(1)} collective-permute-done((bf16[3,32,7168]{2,1,0:T(8,128)(2,1)}, bf16[3,32,7168]{2,1,0:T(8,128)(2,1)S(1)}, u32[]{:S(2)}, u32[]{:S(2)}) %collective-permute-start) | collective-permute-done | bytes 1376288 | tf_op jit(solution)/shard_map/ppermute | solution.py:46
  180.9 0.7 collective-permute-done.2
  181.6 2.6 fusion.12
  184.2 2.4 copy.141
  186.6 7.4 %all-to-all-start.1 = ((bf16[3,32,7168]{2,0,1:T(4,128)(2,1)}), bf16[3,32,7168]{2,0,1:T(4,128)(2,1)S(1)}, u32[]{:S(2)}, u32[]{:S(2)}) async-start(bf16[3,32,7168]{2,0,1:T(4,128)(2,1)} %copy.141), calls=%async_computation.1 | async-start | bytes 3670016 | tf_op jit(solution)/shard_map/all_to_all | solution.py:112
  194.0 0.2 all-gather.11.cloned.1.call-start
  194.3 1.4 select_reduce_fusion.1
  195.8 25.2 %all-to-all-done.1 = bf16[3,32,7168]{2,0,1:T(4,128)(2,1)S(1)} async-done(((bf16[3,32,7168]{2,0,1:T(4,128)(2,1)}), bf16[3,32,7168]{2,0,1:T(4,128)(2,1)S(1)}, u32[]{:S(2)}, u32[]{:S(2)}) %all-to-all-start.1) | async-done | bytes 1376288 | tf_op jit(solution)/shard_map/all_to_all | solution.py:112
  221.0 2.3 multiply_reduce_fusion.1
  223.3 0.8 multiply_convert_fusion
  224.2 0.5 reduce_max.45
  224.8 0.1 copy.172
  225.1 7.1 %fusion.14 = (f32[256,4]{1,0:T(8,128)S(1)}, f32[256,4]{1,0:T(8,128)S(1)}) fusion(bf16[256,4,512]{2,1,0:T(4,128)(2,1)S(1)} %copy-done.3, f32[256,4]{1,0:T(8,128)S(1)} %reduce_max.46, s32[256,4]{1,0:T(8,128)S(1)} %copy.172), kind=kLoop, calls=%fused_computation.25 | loop fusion | flops 3143680 | bytes 1064960 | tf_op jit(solution)/shard_map/reduce_sum | solution.py:82
  232.2 0.1 copy.154
  232.3 0.8 fusion.46
  233.0 88.3 %all-gather.11.cloned.1.call-done = bf16[10,917504]{1,0:T(8,128)(2,1)} async-done(((bf16[10,7168]{1,0:T(8,128)(2,1)}), bf16[10,917504]{1,0:T(8,128)(2,1)}) %all-gather.11.cloned.1.call-update) | async-done | bytes 18350096 | tf_op jit(solution)/shard_map/all_gather | solution.py:119
  321.3 27.4 %copy.176 = bf16[2,8,128,7168]{3,2,1,0:T(8,128)(2,1)} copy(bf16[2,8,128,7168]{3,1,2,0:T(8,128)(2,1)} %bitcast.120) | data formatting | bytes 58720256
  348.7 15.7 %fusion.63 = (f32[10,128]{1,0:T(8,128)S(1)}, f32[10,128,512]{2,1,0:T(8,128)S(1)}) fusion(bf16[512,7168]{1,0:T(8,128)(2,1)} %param.20, bf16[16,128,7168]{2,1,0:T(8,128)(2,1)} %bitcast.121), kind=kOutput, calls=%fused_computation.103 | convolution fusion | flops 9395895296 | bytes 28316672 | tf_op jit(solution)/shard_map/tgd,wd->tgw/dot_general | solution.py:120
  364.4 1.1 exponential_reduce_fusion
  365.5 0.2 copy.146
  365.7 0.2 copy.143
  366.0 0.2 copy.151
  366.3 24.1 %all-gather.1 = f32[48,256,9]{1,2,0:T(8,128)S(1)} all-gather(f32[3,256,9]{1,2,0:T(8,128)S(1)} %pad_maximum_fusion), channel_id=3, replica_groups=mesh['row'=4,'vz'=4,'vx'=4,'core'=2] {'row','vz'}, dimensions={0}, use_global_device_ids=true | all-gather | bytes 470016 | tf_op jit(solution)/shard_map/all_gather | solution.py:26
  390.6 13.5 %all-gather.2 = f32[24,256,9]{1,2,0:T(8,128)S(1)} all-gather(f32[3,256,9]{1,2,0:T(8,128)S(1)} %copy.156), channel_id=4, replica_groups=mesh['row'=4,'vz'=4,'vx'=4,'core'=2] {'vx','core'}, dimensions={0}, use_global_device_ids=true | all-gather | bytes 248832 | tf_op jit(solution)/shard_map/all_gather | solution.py:26
  404.1 1.4 copy.170
  405.5 1.3 bitcast_reduce_fusion
  406.8 1.4 copy.169
  408.2 0.1 copy.174
  408.3 0.1 copy.175
  408.5 1.8 fusion.32
  410.3 0.1 slice_divide_fusion
  410.4 0.1 fusion.45
  410.6 3.9 fusion.19
  414.5 2.2 reduce_sum.164
  416.7 0.1 copy.161
  416.8 0.5 multiply_reduce_fusion
  417.4 0.8 copy-done.5
  418.2 0.2 fusion.34
  418.4 0.1 copy.164
  418.5 0.1 reshape.100
  418.6 21.5 %all-gather.4 = f32[16,1,256]{2,1,0:T(1,128)S(1)} all-gather(f32[1,1,256]{2,1,0:T(1,128)S(1)} %reshape.100), channel_id=1, replica_groups=mesh['row'=4,'vz'=4,'vx'=4,'core'=2] {'row','vz'}, dimensions={0}, use_global_device_ids=true | all-gather | bytes 17408 | tf_op jit(solution)/shard_map/all_gather | solution.py:35
  440.1 10.2 %all-gather.5 = f32[8,1,256]{2,1,0:T(1,128)S(1)} all-gather(f32[1,1,256]{2,1,0:T(1,128)S(1)} %bitcast.142), channel_id=5, replica_groups=mesh['row'=4,'vz'=4,'vx'=4,'core'=2] {'vx','core'}, dimensions={0}, use_global_device_ids=true | all-gather | bytes 9216 | tf_op jit(solution)/shard_map/all_gather | solution.py:35
  450.3 1.4 copy.162
  451.8 0.4 reshape.94
  452.2 0.7 copy.166
  452.8 1.0 divide_sqrt_fusion
  (65 shorter events, 1.2 us)
Async XLA Ops:
  7.2 187.1 %copy-start = (bf16[7168,32]{0,1:T(8,128)(2,1)S(1)}, bf16[7168,32]{0,1:T(8,128)(2,1)}, u32[]{:S(2)}) copy-start(bf16[7168,32]{0,1:T(8,128)(2,1)} %param.14) | copy-start | bytes 1376260
  7.2 97.4 %all-gather.9.cloned.1.call-start = ((), (), s32[]{:S(2)}) async-start(), calls=%async_computation.2 | async-start | bytes 6881280 | tf_op jit(solution)/shard_map/all_gather | solution.py:103
  104.6 5.4 %copy-start.13 = (bf16[3,128,7168]{2,1,0:T(8,128)(2,1)S(1)}, bf16[3,128,7168]{2,1,0:T(8,128)(2,1)}, u32[]{:S(2)}) copy-start(bf16[3,128,7168]{2,1,0:T(8,128)(2,1)} %all-gather.9.cloned.1.call-done) | copy-start | bytes 16515076
  104.6 6.3 %copy-start.14 = (bf16[1,7168,256]{2,1,0:T(8,128)(2,1)S(1)}, bf16[1,7168,256]{2,1,0:T(8,128)(2,1)}, u32[]{:S(2)}) copy-start(bf16[1,7168,256]{2,1,0:T(8,128)(2,1)} %param.17) | copy-start | bytes 11010052
  110.9 2.0 copy-start.7
  114.6 3.6 copy-start.2
  118.2 62.7 %collective-permute-start = (bf16[3,32,7168]{2,1,0:T(8,128)(2,1)}, bf16[3,32,7168]{2,1,0:T(8,128)(2,1)S(1)}, u32[]{:S(2)}, u32[]{:S(2)}) collective-permute-start(bf16[3,32,7168]{2,1,0:T(8,128)(2,1)} %get-tuple-element.14), channel_id=1, source_target_pairs={{0,32},{32,64},{64,96},{96,0},{1,33},{33,65},{65,97},{97,1},{2,34}... | collective-permute-start | bytes 4128776 | tf_op jit(solution)/shard_map/ppermute | solution.py:46
  119.2 61.6 %collective-permute-start.1 = (bf16[3,32,7168]{2,1,0:T(8,128)(2,1)}, bf16[3,32,7168]{2,1,0:T(8,128)(2,1)S(1)}, u32[]{:S(2)}, u32[]{:S(2)}) collective-permute-start(bf16[3,32,7168]{2,1,0:T(8,128)(2,1)} %get-tuple-element.16), channel_id=1, source_target_pairs={{0,64},{32,96},{64,0},{96,32},{1,65},{33,97},{65,1},{97,33},{2,66}... | collective-permute-start | bytes 4128776 | tf_op jit(solution)/shard_map/ppermute | solution.py:46
  120.7 60.8 %collective-permute-start.2 = (bf16[3,32,7168]{2,1,0:T(8,128)(2,1)}, bf16[3,32,7168]{2,1,0:T(8,128)(2,1)}, u32[]{:S(2)}, u32[]{:S(2)}) collective-permute-start(bf16[3,32,7168]{2,1,0:T(8,128)(2,1)} %get-tuple-element.15), channel_id=1, source_target_pairs={{0,96},{32,0},{64,32},{96,64},{1,97},{33,1},{65,33},{97,65},{2,98}... | collective-permute-start | bytes 4128776 | tf_op jit(solution)/shard_map/ppermute | solution.py:46
  186.6 7.6 %copy-start.9 = (f32[7168]{0:T(1024)S(1)}, f32[7168]{0:T(1024)}, u32[]{:S(2)}) copy-start(f32[7168]{0:T(1024)} %param.13) | copy-start | bytes 86020
  186.6 36.7 %copy-start.10 = (f32[7168]{0:T(1024)S(1)}, f32[7168]{0:T(1024)}, u32[]{:S(2)}) copy-start(f32[7168]{0:T(1024)} %param.19) | copy-start | bytes 86020
  186.6 34.4 %all-to-all-start.1 = ((bf16[3,32,7168]{2,0,1:T(4,128)(2,1)}), bf16[3,32,7168]{2,0,1:T(4,128)(2,1)S(1)}, u32[]{:S(2)}, u32[]{:S(2)}) async-start(bf16[3,32,7168]{2,0,1:T(4,128)(2,1)} %copy.141), calls=%async_computation.1 | async-start | bytes 3670016 | tf_op jit(solution)/shard_map/all_to_all | solution.py:112
  194.0 30.2 %copy-start.3 = (bf16[256,4,512]{2,1,0:T(4,128)(2,1)S(1)}, bf16[256,4,512]{2,1,0:T(4,128)(2,1)}, u32[]{:S(2)}) copy-start(bf16[256,4,512]{2,1,0:T(4,128)(2,1)} %param.21) | copy-start | bytes 3145732
  194.0 30.8 %copy-start.12 = (s32[256,4]{0,1:T(4,128)S(1)}, s32[256,4]{0,1:T(4,128)}, u32[]{:S(2)}) copy-start(s32[256,4]{0,1:T(4,128)} %param.22) | copy-start | bytes 12292
  194.0 127.3 %all-gather.11.cloned.1.call-start = ((), (), s32[]{:S(2)}) async-start(), calls=%async_computation.3 | async-start | bytes 29589504 | tf_op jit(solution)/shard_map/all_gather | solution.py:119
  223.3 9.0 %copy-start.11 = (s32[256]{0:T(256)S(1)}, s32[256]{0:T(256)}, u32[]{:S(2)}) copy-start(s32[256]{0:T(256)} %param.23) | copy-start | bytes 3076
  408.5 2.1 copy-start.4
  416.8 1.3 copy-start.8
  416.8 37.1 %copy-start.1 = (bf16[7168,32]{0,1:T(8,128)(2,1)S(1)}, bf16[7168,32]{0,1:T(8,128)(2,1)}, u32[]{:S(2)}) copy-start(bf16[7168,32]{0,1:T(8,128)(2,1)} %param.14) | copy-start | bytes 1376260
  417.4 0.8 copy-start.5
  418.2 34.7 %copy-start.6 = (f32[256,512]{1,0:T(8,128)S(1)}, f32[256,512]{1,0:T(8,128)}, u32[]{:S(2)}) copy-start(f32[256,512]{1,0:T(8,128)} %fusion.19) | copy-start | bytes 1572868
Sparse Core Ops, SparseCore 0:
  47.7 56.8 all-gather.8
  224.3 96.9 all-gather.10
where the time goes:
time: 463 us; the launch traced here: 461 us
  waiting for transfers between devices  229 us (49%)
  blocking collectives  103 us (22%)
  local copies, waits for them, and re-layouts  48.6 us (10%)
  matrix products  29.5 us (6%)
  other arithmetic  23.5 us (5%)
  between operations  14.5 us (3%)
  starting transfers between devices  12.5 us (3%)
    all_gather x1, waiting for transfers between devices, body(): gathered = lax.all_gather(final_normed, ALL_AXES, axis=1, tiled=False)  88.3 us
    ppermute x3, waiting for transfers between devices, row_reduce_scatter(): total = total + lax.ppermute(chunk, 'row', pairs).astype(jnp.float32)  58.5 us
    all_gather x1, waiting for transfers between devices, body(): shard_piece = lax.all_gather(received, 'row', axis=1, tiled=True)  57 us
    all_gather x2, blocking collectives, merged_stats(): every = lax.all_gather(payload, axes, axis=0, tiled=False)  37.5 us
    unnamed x39, local copies, waits for them, and re-layouts  35.9 us
    all_to_all x1, blocking collectives, body(): lax.all_to_all(send_buffer, VOCAB_AXES, split_axis=1, concat_axis=1, tile...  33.8 us
    all_gather x2, blocking collectives, gathered_sum(): values = jnp.sum(lax.all_gather(values, axes, axis=0, tiled=False), axis=0)  31.7 us
    all_to_all x1, waiting for transfers between devices, body(): lax.all_to_all(summed, VOCAB_AXES, split_axis=1, concat_axis=1, tiled=True)  25.2 us
  transfers between devices with their start and end apart: 6, of which 5 were waited for; matrix products, arithmetic and copies ran while one was open for 2% of the time, Pallas kernels for 0%

commit v1 on v0

--- a/solution.py
+++ b/solution.py
@@ -116,10 +116,13 @@
     )
     mixed_rows = resid_in + moe_sum
     final_normed = rms_norm(mixed_rows, head_gain).astype(jnp.bfloat16)
-    gathered = lax.all_gather(final_normed, ALL_AXES, axis=1, tiled=False)
-    logits = jnp.einsum("tgd,wd->tgw", gathered, head, preferred_element_type=jnp.float32)
     halves = rows_dev // slot_total
-    target_logits = logits.reshape(halves, slot_total, -1, local_vocab)
+    parts = []
+    for half in range(halves):
+        piece = final_normed[half * slot_total:(half + 1) * slot_total]
+        gathered = lax.all_gather(piece, ALL_AXES, axis=1, tiled=False)
+        parts.append(jnp.einsum("tgd,wd->tgw", gathered, head, preferred_element_type=jnp.float32))
+    target_logits = jnp.stack(parts)
 
     def to_requests(values):
         return jnp.transpose(values, (2, 0, 1)).reshape(requests, slot_total)

time: 463 us -> 491 us (1.060)
  waiting for transfers between devices: 229 us -> 270 us
  local copies, waits for them, and re-layouts: 48.6 us -> 22 us
  matrix products: 29.5 us -> 43.9 us
    all_gather x1 -> x2, waiting for transfers between devices: 88.3 us -> 128 us  [body(): gathered = lax.all_gather(piece, ALL_AXES, axis=1, tiled=False)]
    unnamed x39 -> x38, local copies, waits for them, and re-layouts: 35.9 us -> 8.5 us
    dot_general x1 -> x2, matrix products: 15.7 us -> 30.1 us  [body(): jnp.einsum('tgd,wd->tgw', gathered, head, preferred_element_type=jnp.floa...]
  transfers between devices with their start and end apart: 6 -> 7, of which waited for: 5 -> 6; matrix products, arithmetic and copies ran while one was open for 2% -> 5% of each run, Pallas kernels for 0% -> 0%
where the time goes in v1:
time: 491 us; the launch traced here: 489 us
  waiting for transfers between devices  270 us (55%)
  blocking collectives  103 us (21%)
  matrix products  43.9 us (9%)
  other arithmetic  23.6 us (5%)
  local copies, waits for them, and re-layouts  22 us (4%)
  between operations  14.2 us (3%)
  starting transfers between devices  12.4 us (3%)
    all_gather x2, waiting for transfers between devices, body(): gathered = lax.all_gather(piece, ALL_AXES, axis=1, tiled=False)  128 us
    ppermute x3, waiting for transfers between devices, row_reduce_scatter(): total = total + lax.ppermute(chunk, 'row', pairs).astype(jnp.float32)  58.5 us
    all_gather x1, waiting for transfers between devices, body(): shard_piece = lax.all_gather(received, 'row', axis=1, tiled=True)  57 us
    all_gather x2, blocking collectives, merged_stats(): every = lax.all_gather(payload, axes, axis=0, tiled=False)  37.3 us
    all_to_all x1, blocking collectives, body(): lax.all_to_all(send_buffer, VOCAB_AXES, split_axis=1, concat_axis=1, tile...  33.8 us
    all_gather x2, blocking collectives, gathered_sum(): values = jnp.sum(lax.all_gather(values, axes, axis=0, tiled=False), axis=0)  31.6 us
    dot_general x2, matrix products, body(): jnp.einsum('tgd,wd->tgw', gathered, head, preferred_element_type=jnp.floa...  30.1 us
    all_to_all x1, waiting for transfers between devices, body(): lax.all_to_all(summed, VOCAB_AXES, split_axis=1, concat_axis=1, tiled=True)  25.4 us
  transfers between devices with their start and end apart: 7, of which 6 were waited for; matrix products, arithmetic and copies ran while one was open for 5% of the time, Pallas kernels for 0%

profile of v1, /device:TPU:0, one launch (start us, length us, event | category | flops | bytes accessed | tf_op | source)
XLA Modules:
  0.0 488.6 jit_solution(14184808900583214998)
XLA Ops:
  7.2 0.8 copy.135
  8.2 1.1 fusion.51
  9.3 1.5 fusion.6
  10.8 1.2 copy.136
  12.0 33.8 %all_to_all.10 = bf16[3,32,7168]{2,0,1:T(4,128)(2,1)S(1)} all-to-all(bf16[3,32,7168]{2,0,1:T(4,128)(2,1)S(1)} %copy.136), channel_id=1, replica_groups=mesh['row'=4,'vz'=4,'vx'=4,'core'=2] {'vz','vx','core'}, dimensions={1} | all-to-all | bytes 2752512 | tf_op jit(solution)/shard_map/all_to_all | solution.py:102
  45.9 1.7 copy.137
  47.6 57.0 %all-gather.11.cloned.1.call-done = bf16[3,128,7168]{2,1,0:T(8,128)(2,1)} async-done(((bf16[3,32,7168]{2,1,0:T(8,128)(2,1)}), bf16[3,128,7168]{2,1,0:T(8,128)(2,1)}) %all-gather.11.cloned.1.call-update) | async-done | bytes 5505040 | tf_op jit(solution)/shard_map/all_gather | solution.py:103
  104.6 5.4 %fusion.13 = f32[384,256]{1,0:T(8,128)S(1)} fusion(bf16[384,7168]{1,0:T(8,128)(2,1)} %bitcast.158, bf16[1,7168,256]{2,1,0:T(8,128)(2,1)} %param.16), kind=kOutput, calls=%fused_computation.16 | convolution fusion | flops 1409286144 | bytes 9568256 | tf_op jit(solution)/shard_map/dot_general | solution.py:105
  110.0 0.9 copy-done.14
  110.9 1.6 fusion.40
  112.5 0.4 copy-done.7
  113.0 1.6 convolution_convert_fusion
  114.6 2.1 dynamic-slice_bitcast_fusion.2
  116.7 1.5 copy-done.2
  118.2 1.0 collective-permute-start
  119.2 1.5 collective-permute-start.1
  120.7 2.3 collective-permute-start.2
  123.1 57.8 %collective-permute-done = bf16[3,32,7168]{2,1,0:T(8,128)(2,1)S(1)} collective-permute-done((bf16[3,32,7168]{2,1,0:T(8,128)(2,1)}, bf16[3,32,7168]{2,1,0:T(8,128)(2,1)S(1)}, u32[]{:S(2)}, u32[]{:S(2)}) %collective-permute-start) | collective-permute-done | bytes 1376288 | tf_op jit(solution)/shard_map/ppermute | solution.py:46
  180.9 0.7 collective-permute-done.2
  181.6 2.6 fusion.17
  184.2 2.4 copy.139
  186.6 7.4 %all-to-all-start.1 = ((bf16[3,32,7168]{2,0,1:T(4,128)(2,1)}), bf16[3,32,7168]{2,0,1:T(4,128)(2,1)S(1)}, u32[]{:S(2)}, u32[]{:S(2)}) async-start(bf16[3,32,7168]{2,0,1:T(4,128)(2,1)} %copy.139), calls=%async_computation.1 | async-start | bytes 3670016 | tf_op jit(solution)/shard_map/all_to_all | solution.py:112
  194.1 1.4 select_reduce_fusion.1
  195.6 25.4 %all-to-all-done.1 = bf16[3,32,7168]{2,0,1:T(4,128)(2,1)S(1)} async-done(((bf16[3,32,7168]{2,0,1:T(4,128)(2,1)}), bf16[3,32,7168]{2,0,1:T(4,128)(2,1)S(1)}, u32[]{:S(2)}, u32[]{:S(2)}) %all-to-all-start.1) | async-done | bytes 1376288 | tf_op jit(solution)/shard_map/all_to_all | solution.py:112
  221.0 2.3 multiply_reduce_fusion.1
  223.3 0.1 multiply_convert_fusion
  223.5 0.7 fusion.78
  224.3 0.7 all-gather.15.cloned.1.call-update
  225.0 0.5 reduce_max.42
  225.6 0.1 copy.170
  225.8 7.2 %fusion.19 = (f32[256,4]{1,0:T(8,128)S(1)}, f32[256,4]{1,0:T(8,128)S(1)}) fusion(bf16[256,4,512]{2,1,0:T(4,128)(2,1)S(1)} %copy-done.3, f32[256,4]{1,0:T(8,128)S(1)} %reduce_max.43, s32[256,4]{1,0:T(8,128)S(1)} %copy.170), kind=kLoop, calls=%fused_computation.31 | loop fusion | flops 3143680 | bytes 1064960 | tf_op jit(solution)/shard_map/reduce_sum | solution.py:82
  233.2 0.8 fusion.62
  234.0 64.0 %all-gather.13.cloned.1.call-done = bf16[5,917504]{1,0:T(8,128)(2,1)} async-done(((bf16[5,7168]{1,0:T(8,128)(2,1)}), bf16[5,917504]{1,0:T(8,128)(2,1)}) %all-gather.13.cloned.1.call-update) | async-done | bytes 9175056 | tf_op jit(solution)/shard_map/all_gather | solution.py:123
  298.0 15.0 %fusion.25 = f32[1,5,128,512]{3,2,1,0:T(8,128)S(1)} fusion(bf16[512,7168]{1,0:T(8,128)(2,1)} %param.20, bf16[1,5,128,7168]{3,1,2,0:T(8,128)(2,1)} %bitcast.156), kind=kOutput, calls=%fused_computation.38 | convolution fusion | flops 4697620480 | bytes 17825792 | tf_op jit(solution)/shard_map/tgd,wd->tgw/dot_general | solution.py:124
  313.0 64.1 %all-gather.15.cloned.1.call-done = bf16[5,917504]{1,0:T(8,128)(2,1)} async-done(((bf16[5,7168]{1,0:T(8,128)(2,1)}), bf16[5,917504]{1,0:T(8,128)(2,1)}) %all-gather.15.cloned.1.call-update) | async-done | bytes 9175056 | tf_op jit(solution)/shard_map/all_gather | solution.py:123
  377.1 15.0 %fusion.30 = f32[1,5,128,512]{3,2,1,0:T(8,128)S(1)} fusion(bf16[512,7168]{1,0:T(8,128)(2,1)} %param.20, bf16[1,5,128,7168]{3,1,2,0:T(8,128)(2,1)} %bitcast.157), kind=kOutput, calls=%fused_computation.39 | convolution fusion | flops 4697620480 | bytes 17825792 | tf_op jit(solution)/shard_map/tgd,wd->tgw/dot_general | solution.py:124
  392.2 0.2 fusion.36
  392.4 1.5 exponential_reduce_fusion
  393.9 0.2 copy.144
  394.1 0.2 copy.141
  394.4 0.2 copy.149
  394.7 24.0 %all-gather.2 = f32[48,256,9]{1,2,0:T(8,128)S(1)} all-gather(f32[3,256,9]{1,2,0:T(8,128)S(1)} %pad_maximum_fusion.1), channel_id=4, replica_groups=mesh['row'=4,'vz'=4,'vx'=4,'core'=2] {'row','vz'}, dimensions={0}, use_global_device_ids=true | all-gather | bytes 470016 | tf_op jit(solution)/shard_map/all_gather | solution.py:26
  418.9 13.4 %all-gather.3 = f32[24,256,9]{1,2,0:T(8,128)S(1)} all-gather(f32[3,256,9]{1,2,0:T(8,128)S(1)} %copy.154), channel_id=5, replica_groups=mesh['row'=4,'vz'=4,'vx'=4,'core'=2] {'vx','core'}, dimensions={0}, use_global_device_ids=true | all-gather | bytes 248832 | tf_op jit(solution)/shard_map/all_gather | solution.py:26
  432.3 1.4 copy.168
  433.6 1.3 bitcast_reduce_fusion
  435.0 1.4 copy.167
  436.4 0.1 copy.172
  436.5 0.1 copy.173
  436.7 1.8 fusion.48
  438.5 0.1 slice_divide_fusion
  438.6 0.1 fusion.61
  438.8 3.9 fusion.24
  442.7 2.2 reduce_sum.158
  445.0 0.5 multiply_reduce_fusion
  445.5 0.8 copy-done.5
  446.3 0.2 fusion.50
  446.5 0.1 copy.162
  446.7 0.1 reshape.89
  446.8 22.0 %all-gather.5 = f32[16,1,256]{2,1,0:T(1,128)S(1)} all-gather(f32[1,1,256]{2,1,0:T(1,128)S(1)} %reshape.89), channel_id=1, replica_groups=mesh['row'=4,'vz'=4,'vx'=4,'core'=2] {'row','vz'}, dimensions={0}, use_global_device_ids=true | all-gather | bytes 17408 | tf_op jit(solution)/shard_map/all_gather | solution.py:35
  468.9 9.6 %all-gather.6 = f32[8,1,256]{2,1,0:T(1,128)S(1)} all-gather(f32[1,1,256]{2,1,0:T(1,128)S(1)} %bitcast.155), channel_id=6, replica_groups=mesh['row'=4,'vz'=4,'vx'=4,'core'=2] {'vx','core'}, dimensions={0}, use_global_device_ids=true | all-gather | bytes 9216 | tf_op jit(solution)/shard_map/all_gather | solution.py:35
  478.5 1.4 copy.160
  480.0 0.4 reshape.82
  480.3 0.7 copy.164
  481.0 1.0 divide_sqrt_fusion
  (66 shorter events, 1.5 us)
Async XLA Ops:
  7.2 186.9 %copy-start = (bf16[7168,32]{0,1:T(8,128)(2,1)S(1)}, bf16[7168,32]{0,1:T(8,128)(2,1)}, u32[]{:S(2)}) copy-start(bf16[7168,32]{0,1:T(8,128)(2,1)} %param.14) | copy-start | bytes 1376260
  7.2 97.4 %all-gather.11.cloned.1.call-start = ((), (), s32[]{:S(2)}) async-start(), calls=%async_computation.2 | async-start | bytes 6881280 | tf_op jit(solution)/shard_map/all_gather | solution.py:103
  104.6 5.4 %copy-start.13 = (bf16[3,128,7168]{2,1,0:T(8,128)(2,1)S(1)}, bf16[3,128,7168]{2,1,0:T(8,128)(2,1)}, u32[]{:S(2)}) copy-start(bf16[3,128,7168]{2,1,0:T(8,128)(2,1)} %all-gather.11.cloned.1.call-done) | copy-start | bytes 16515076
  104.6 6.3 %copy-start.14 = (bf16[1,7168,256]{2,1,0:T(8,128)(2,1)S(1)}, bf16[1,7168,256]{2,1,0:T(8,128)(2,1)}, u32[]{:S(2)}) copy-start(bf16[1,7168,256]{2,1,0:T(8,128)(2,1)} %param.17) | copy-start | bytes 11010052
  110.9 2.0 copy-start.7
  114.6 3.6 copy-start.2
  118.2 62.7 %collective-permute-start = (bf16[3,32,7168]{2,1,0:T(8,128)(2,1)}, bf16[3,32,7168]{2,1,0:T(8,128)(2,1)S(1)}, u32[]{:S(2)}, u32[]{:S(2)}) collective-permute-start(bf16[3,32,7168]{2,1,0:T(8,128)(2,1)} %get-tuple-element.14), channel_id=1, source_target_pairs={{0,32},{32,64},{64,96},{96,0},{1,33},{33,65},{65,97},{97,1},{2,34}... | collective-permute-start | bytes 4128776 | tf_op jit(solution)/shard_map/ppermute | solution.py:46
  119.2 61.6 %collective-permute-start.1 = (bf16[3,32,7168]{2,1,0:T(8,128)(2,1)}, bf16[3,32,7168]{2,1,0:T(8,128)(2,1)S(1)}, u32[]{:S(2)}, u32[]{:S(2)}) collective-permute-start(bf16[3,32,7168]{2,1,0:T(8,128)(2,1)} %get-tuple-element.16), channel_id=1, source_target_pairs={{0,64},{32,96},{64,0},{96,32},{1,65},{33,97},{65,1},{97,33},{2,66}... | collective-permute-start | bytes 4128776 | tf_op jit(solution)/shard_map/ppermute | solution.py:46
  120.7 60.8 %collective-permute-start.2 = (bf16[3,32,7168]{2,1,0:T(8,128)(2,1)}, bf16[3,32,7168]{2,1,0:T(8,128)(2,1)}, u32[]{:S(2)}, u32[]{:S(2)}) collective-permute-start(bf16[3,32,7168]{2,1,0:T(8,128)(2,1)} %get-tuple-element.15), channel_id=1, source_target_pairs={{0,96},{32,0},{64,32},{96,64},{1,97},{33,1},{65,33},{97,65},{2,98}... | collective-permute-start | bytes 4128776 | tf_op jit(solution)/shard_map/ppermute | solution.py:46
  186.6 7.4 %copy-start.9 = (f32[7168]{0:T(1024)S(1)}, f32[7168]{0:T(1024)}, u32[]{:S(2)}) copy-start(f32[7168]{0:T(1024)} %param.13) | copy-start | bytes 86020
  186.6 36.7 %copy-start.10 = (f32[7168]{0:T(1024)S(1)}, f32[7168]{0:T(1024)}, u32[]{:S(2)}) copy-start(f32[7168]{0:T(1024)} %param.19) | copy-start | bytes 86020
  186.6 34.4 %all-to-all-start.1 = ((bf16[3,32,7168]{2,0,1:T(4,128)(2,1)}), bf16[3,32,7168]{2,0,1:T(4,128)(2,1)S(1)}, u32[]{:S(2)}, u32[]{:S(2)}) async-start(bf16[3,32,7168]{2,0,1:T(4,128)(2,1)} %copy.139), calls=%async_computation.1 | async-start | bytes 3670016 | tf_op jit(solution)/shard_map/all_to_all | solution.py:112
  194.0 31.0 %copy-start.3 = (bf16[256,4,512]{2,1,0:T(4,128)(2,1)S(1)}, bf16[256,4,512]{2,1,0:T(4,128)(2,1)}, u32[]{:S(2)}) copy-start(bf16[256,4,512]{2,1,0:T(4,128)(2,1)} %param.21) | copy-start | bytes 3145732
  194.0 104.0 %all-gather.13.cloned.1.call-start = ((), (), s32[]{:S(2)}) async-start(), calls=%async_computation.3 | async-start | bytes 14794752 | tf_op jit(solution)/shard_map/all_gather | solution.py:123
  195.5 30.1 %copy-start.12 = (s32[256,4]{0,1:T(4,128)S(1)}, s32[256,4]{0,1:T(4,128)}, u32[]{:S(2)}) copy-start(s32[256,4]{0,1:T(4,128)} %param.22) | copy-start | bytes 12292
  223.3 9.9 %copy-start.11 = (s32[256]{0:T(256)S(1)}, s32[256]{0:T(256)}, u32[]{:S(2)}) copy-start(s32[256]{0:T(256)} %param.23) | copy-start | bytes 3076
  224.2 152.9 %all-gather.15.cloned.1.call-start = ((), (), s32[]{:S(2)}) async-start(), calls=%async_computation.4 | async-start | bytes 14794752 | tf_op jit(solution)/shard_map/all_gather | solution.py:123
  436.6 2.1 copy-start.4
  445.0 1.3 copy-start.8
  445.0 37.0 %copy-start.1 = (bf16[7168,32]{0,1:T(8,128)(2,1)S(1)}, bf16[7168,32]{0,1:T(8,128)(2,1)}, u32[]{:S(2)}) copy-start(bf16[7168,32]{0,1:T(8,128)(2,1)} %param.14) | copy-start | bytes 1376260
  445.5 0.8 copy-start.5
  446.3 34.7 %copy-start.6 = (f32[256,512]{1,0:T(8,128)S(1)}, f32[256,512]{1,0:T(8,128)}, u32[]{:S(2)}) copy-start(f32[256,512]{1,0:T(8,128)} %fusion.24) | copy-start | bytes 1572868
Sparse Core Ops, SparseCore 0:
  47.7 56.8 all-gather.10
  224.3 73.5 all-gather.12
  301.0 76.1 all-gather.14

commit v2 on v0

--- a/solution.py
+++ b/solution.py
@@ -116,10 +116,19 @@
     )
     mixed_rows = resid_in + moe_sum
     final_normed = rms_norm(mixed_rows, head_gain).astype(jnp.bfloat16)
+    halves = rows_dev // slot_total
     gathered = lax.all_gather(final_normed, ALL_AXES, axis=1, tiled=False)
-    logits = jnp.einsum("tgd,wd->tgw", gathered, head, preferred_element_type=jnp.float32)
-    halves = rows_dev // slot_total
-    target_logits = logits.reshape(halves, slot_total, -1, local_vocab)
+    target_logits = jnp.stack(
+        [
+            jnp.einsum(
+                "tgd,wd->tgw",
+                gathered[half * slot_total:(half + 1) * slot_total],
+                head,
+                preferred_element_type=jnp.float32,
+            )
+            for half in range(halves)
+        ]
+    )
 
     def to_requests(values):
         return jnp.transpose(values, (2, 0, 1)).reshape(requests, slot_total)

time: 463 us -> 475 us (1.026)
  matrix products: 29.5 us -> 44 us
    unnamed x39 -> x38, local copies, waits for them, and re-layouts: 35.9 us -> 8.5 us
    slice x0 -> x1, local copies, waits for them, and re-layouts: none -> 25.2 us  [body(): gathered[half * slot_total:(half + 1) * slot_total]]
    dot_general x1 -> x2, matrix products: 15.7 us -> 30.1 us  [body(): jnp.einsum('tgd,wd->tgw', gathered[half * slot_total:(half + 1) * slot_to...]
where the time goes in v2:
time: 475 us; the launch traced here: 473 us
  waiting for transfers between devices  229 us (48%)
  blocking collectives  103 us (22%)
  local copies, waits for them, and re-layouts  46.5 us (10%)
  matrix products  44 us (9%)
  other arithmetic  24.2 us (5%)
  between operations  14.5 us (3%)
  starting transfers between devices  12.3 us (3%)
    all_gather x1, waiting for transfers between devices, body(): gathered = lax.all_gather(final_normed, ALL_AXES, axis=1, tiled=False)  88.1 us
    ppermute x3, waiting for transfers between devices, row_reduce_scatter(): total = total + lax.ppermute(chunk, 'row', pairs).astype(jnp.float32)  58.5 us
    all_gather x1, waiting for transfers between devices, body(): shard_piece = lax.all_gather(received, 'row', axis=1, tiled=True)  57 us
    all_gather x2, blocking collectives, merged_stats(): every = lax.all_gather(payload, axes, axis=0, tiled=False)  37.3 us
    all_to_all x1, blocking collectives, body(): lax.all_to_all(send_buffer, VOCAB_AXES, split_axis=1, concat_axis=1, tile...  33.8 us
    all_gather x2, blocking collectives, gathered_sum(): values = jnp.sum(lax.all_gather(values, axes, axis=0, tiled=False), axis=0)  31.7 us
    dot_general x2, matrix products, body(): jnp.einsum('tgd,wd->tgw', gathered[half * slot_total:(half + 1) * slot_to...  30.1 us
    all_to_all x1, waiting for transfers between devices, body(): lax.all_to_all(summed, VOCAB_AXES, split_axis=1, concat_axis=1, tiled=True)  25.4 us
  transfers between devices with their start and end apart: 6, of which 5 were waited for; matrix products, arithmetic and copies ran while one was open for 2% of the time, Pallas kernels for 0%

profile of v2, /device:TPU:0, one launch (start us, length us, event | category | flops | bytes accessed | tf_op | source)
XLA Modules:
  0.0 473.4 jit_solution(13003443471366593902)
XLA Ops:
  7.2 0.8 copy.135
  8.0 0.1 fusion.65
  8.2 1.1 fusion.51
  9.3 1.5 fusion.6
  10.8 1.2 copy.136
  12.0 33.8 %all_to_all.10 = bf16[3,32,7168]{2,0,1:T(4,128)(2,1)S(1)} all-to-all(bf16[3,32,7168]{2,0,1:T(4,128)(2,1)S(1)} %copy.136), channel_id=1, replica_groups=mesh['row'=4,'vz'=4,'vx'=4,'core'=2] {'vz','vx','core'}, dimensions={1} | all-to-all | bytes 2752512 | tf_op jit(solution)/shard_map/all_to_all | solution.py:102
  45.9 1.7 copy.137
  47.6 57.0 %all-gather.9.cloned.1.call-done = bf16[3,128,7168]{2,1,0:T(8,128)(2,1)} async-done(((bf16[3,32,7168]{2,1,0:T(8,128)(2,1)}), bf16[3,128,7168]{2,1,0:T(8,128)(2,1)}) %all-gather.9.cloned.1.call-update) | async-done | bytes 5505040 | tf_op jit(solution)/shard_map/all_gather | solution.py:103
  104.6 5.4 %fusion.13 = f32[384,256]{1,0:T(8,128)S(1)} fusion(bf16[384,7168]{1,0:T(8,128)(2,1)} %bitcast.158, bf16[1,7168,256]{2,1,0:T(8,128)(2,1)} %param.16), kind=kOutput, calls=%fused_computation.16 | convolution fusion | flops 1409286144 | bytes 9568256 | tf_op jit(solution)/shard_map/dot_general | solution.py:105
  110.0 0.9 copy-done.14
  110.9 1.6 fusion.40
  112.5 0.4 copy-done.7
  113.0 1.6 convolution_convert_fusion
  114.6 2.1 dynamic-slice_bitcast_fusion.2
  116.7 1.5 copy-done.2
  118.2 1.0 collective-permute-start
  119.2 1.5 collective-permute-start.1
  120.7 2.3 collective-permute-start.2
  123.1 57.8 %collective-permute-done = bf16[3,32,7168]{2,1,0:T(8,128)(2,1)S(1)} collective-permute-done((bf16[3,32,7168]{2,1,0:T(8,128)(2,1)}, bf16[3,32,7168]{2,1,0:T(8,128)(2,1)S(1)}, u32[]{:S(2)}, u32[]{:S(2)}) %collective-permute-start) | collective-permute-done | bytes 1376288 | tf_op jit(solution)/shard_map/ppermute | solution.py:46
  180.9 0.7 collective-permute-done.2
  181.6 2.6 fusion.17
  184.2 2.4 copy.139
  186.6 7.4 %all-to-all-start.1 = ((bf16[3,32,7168]{2,0,1:T(4,128)(2,1)}), bf16[3,32,7168]{2,0,1:T(4,128)(2,1)S(1)}, u32[]{:S(2)}, u32[]{:S(2)}) async-start(bf16[3,32,7168]{2,0,1:T(4,128)(2,1)} %copy.139), calls=%async_computation.1 | async-start | bytes 3670016 | tf_op jit(solution)/shard_map/all_to_all | solution.py:112
  194.1 1.4 select_reduce_fusion.1
  195.6 25.4 %all-to-all-done.1 = bf16[3,32,7168]{2,0,1:T(4,128)(2,1)S(1)} async-done(((bf16[3,32,7168]{2,0,1:T(4,128)(2,1)}), bf16[3,32,7168]{2,0,1:T(4,128)(2,1)S(1)}, u32[]{:S(2)}, u32[]{:S(2)}) %all-to-all-start.1) | async-done | bytes 1376288 | tf_op jit(solution)/shard_map/all_to_all | solution.py:112
  221.0 2.3 multiply_reduce_fusion.1
  223.3 0.8 multiply_convert_fusion
  224.2 0.5 reduce_max.42
  224.8 0.1 copy.170
  225.1 7.2 %fusion.19 = (f32[256,4]{1,0:T(8,128)S(1)}, f32[256,4]{1,0:T(8,128)S(1)}) fusion(bf16[256,4,512]{2,1,0:T(4,128)(2,1)S(1)} %copy-done.3, f32[256,4]{1,0:T(8,128)S(1)} %reduce_max.43, s32[256,4]{1,0:T(8,128)S(1)} %copy.170), kind=kLoop, calls=%fused_computation.31 | loop fusion | flops 3143680 | bytes 1064960 | tf_op jit(solution)/shard_map/reduce_sum | solution.py:82
  232.5 0.8 fusion.62
  233.2 88.1 %all-gather.11.cloned.1.call-done = bf16[10,917504]{1,0:T(8,128)(2,1)} async-done(((bf16[10,7168]{1,0:T(8,128)(2,1)}), bf16[10,917504]{1,0:T(8,128)(2,1)}) %all-gather.11.cloned.1.call-update) | async-done | bytes 18350096 | tf_op jit(solution)/shard_map/all_gather | solution.py:120
  321.3 25.2 %fusion.78 = (bf16[5,917504]{1,0:T(8,128)(2,1)}, bf16[5,917504]{1,0:T(8,128)(2,1)}) fusion(bf16[10,917504]{1,0:T(8,128)(2,1)} %all-gather.11.cloned.1.call-done), kind=kLoop, calls=%fused_computation.111 | loop fusion | bytes 36700160 | tf_op jit(solution)/shard_map/slice | solution.py:125
  346.5 15.1 %fusion.25 = f32[1,5,128,512]{3,2,1,0:T(8,128)S(1)} fusion(bf16[512,7168]{1,0:T(8,128)(2,1)} %param.20, bf16[1,5,128,7168]{3,1,2,0:T(8,128)(2,1)} %bitcast.139), kind=kOutput, calls=%fused_computation.38 | convolution fusion | flops 4697620480 | bytes 17825792 | tf_op jit(solution)/shard_map/tgd,wd->tgw/dot_general | solution.py:123
  361.6 15.1 %fusion.30 = f32[1,5,128,512]{3,2,1,0:T(8,128)S(1)} fusion(bf16[512,7168]{1,0:T(8,128)(2,1)} %param.20, bf16[1,5,128,7168]{3,1,2,0:T(8,128)(2,1)} %bitcast.138), kind=kOutput, calls=%fused_computation.39 | convolution fusion | flops 4697620480 | bytes 17825792 | tf_op jit(solution)/shard_map/tgd,wd->tgw/dot_general | solution.py:123
  376.7 0.2 fusion.36
  376.9 1.5 exponential_reduce_fusion
  378.4 0.2 copy.144
  378.6 0.2 copy.141
  378.9 0.2 copy.149
  379.2 24.1 %all-gather.1 = f32[48,256,9]{1,2,0:T(8,128)S(1)} all-gather(f32[3,256,9]{1,2,0:T(8,128)S(1)} %pad_maximum_fusion.1), channel_id=3, replica_groups=mesh['row'=4,'vz'=4,'vx'=4,'core'=2] {'row','vz'}, dimensions={0}, use_global_device_ids=true | all-gather | bytes 470016 | tf_op jit(solution)/shard_map/all_gather | solution.py:26
  403.5 13.2 %all-gather.2 = f32[24,256,9]{1,2,0:T(8,128)S(1)} all-gather(f32[3,256,9]{1,2,0:T(8,128)S(1)} %copy.154), channel_id=4, replica_groups=mesh['row'=4,'vz'=4,'vx'=4,'core'=2] {'vx','core'}, dimensions={0}, use_global_device_ids=true | all-gather | bytes 248832 | tf_op jit(solution)/shard_map/all_gather | solution.py:26
  416.8 1.4 copy.168
  418.1 1.3 bitcast_reduce_fusion
  419.4 1.4 copy.167
  420.8 0.1 copy.172
  421.0 0.1 copy.173
  421.1 1.8 fusion.48
  423.0 0.1 slice_divide_fusion
  423.1 0.1 fusion.61
  423.3 3.9 fusion.24
  427.2 2.2 reduce_sum.158
  429.4 0.1 copy.159
  429.5 0.5 multiply_reduce_fusion
  430.0 0.8 copy-done.5
  430.8 0.2 fusion.50
  431.0 0.1 copy.162
  431.1 0.1 reshape.90
  431.3 21.5 %all-gather.4 = f32[16,1,256]{2,1,0:T(1,128)S(1)} all-gather(f32[1,1,256]{2,1,0:T(1,128)S(1)} %reshape.90), channel_id=1, replica_groups=mesh['row'=4,'vz'=4,'vx'=4,'core'=2] {'row','vz'}, dimensions={0}, use_global_device_ids=true | all-gather | bytes 17408 | tf_op jit(solution)/shard_map/all_gather | solution.py:35
  452.8 10.2 %all-gather.5 = f32[8,1,256]{2,1,0:T(1,128)S(1)} all-gather(f32[1,1,256]{2,1,0:T(1,128)S(1)} %bitcast.157), channel_id=5, replica_groups=mesh['row'=4,'vz'=4,'vx'=4,'core'=2] {'vx','core'}, dimensions={0}, use_global_device_ids=true | all-gather | bytes 9216 | tf_op jit(solution)/shard_map/all_gather | solution.py:35
  463.0 1.4 copy.160
  464.5 0.4 reshape.82
  464.8 0.7 copy.164
  465.5 1.0 divide_sqrt_fusion
  (63 shorter events, 1.3 us)
Async XLA Ops:
  7.2 186.9 %copy-start = (bf16[7168,32]{0,1:T(8,128)(2,1)S(1)}, bf16[7168,32]{0,1:T(8,128)(2,1)}, u32[]{:S(2)}) copy-start(bf16[7168,32]{0,1:T(8,128)(2,1)} %param.14) | copy-start | bytes 1376260
  7.2 97.4 %all-gather.9.cloned.1.call-start = ((), (), s32[]{:S(2)}) async-start(), calls=%async_computation.2 | async-start | bytes 6881280 | tf_op jit(solution)/shard_map/all_gather | solution.py:103
  104.6 5.4 %copy-start.13 = (bf16[3,128,7168]{2,1,0:T(8,128)(2,1)S(1)}, bf16[3,128,7168]{2,1,0:T(8,128)(2,1)}, u32[]{:S(2)}) copy-start(bf16[3,128,7168]{2,1,0:T(8,128)(2,1)} %all-gather.9.cloned.1.call-done) | copy-start | bytes 16515076
  104.6 6.3 %copy-start.14 = (bf16[1,7168,256]{2,1,0:T(8,128)(2,1)S(1)}, bf16[1,7168,256]{2,1,0:T(8,128)(2,1)}, u32[]{:S(2)}) copy-start(bf16[1,7168,256]{2,1,0:T(8,128)(2,1)} %param.17) | copy-start | bytes 11010052
  110.9 2.0 copy-start.7
  114.6 3.6 copy-start.2
  118.2 62.7 %collective-permute-start = (bf16[3,32,7168]{2,1,0:T(8,128)(2,1)}, bf16[3,32,7168]{2,1,0:T(8,128)(2,1)S(1)}, u32[]{:S(2)}, u32[]{:S(2)}) collective-permute-start(bf16[3,32,7168]{2,1,0:T(8,128)(2,1)} %get-tuple-element.16), channel_id=1, source_target_pairs={{0,32},{32,64},{64,96},{96,0},{1,33},{33,65},{65,97},{97,1},{2,34}... | collective-permute-start | bytes 4128776 | tf_op jit(solution)/shard_map/ppermute | solution.py:46
  119.2 61.6 %collective-permute-start.1 = (bf16[3,32,7168]{2,1,0:T(8,128)(2,1)}, bf16[3,32,7168]{2,1,0:T(8,128)(2,1)S(1)}, u32[]{:S(2)}, u32[]{:S(2)}) collective-permute-start(bf16[3,32,7168]{2,1,0:T(8,128)(2,1)} %get-tuple-element.18), channel_id=1, source_target_pairs={{0,64},{32,96},{64,0},{96,32},{1,65},{33,97},{65,1},{97,33},{2,66}... | collective-permute-start | bytes 4128776 | tf_op jit(solution)/shard_map/ppermute | solution.py:46
  120.7 60.8 %collective-permute-start.2 = (bf16[3,32,7168]{2,1,0:T(8,128)(2,1)}, bf16[3,32,7168]{2,1,0:T(8,128)(2,1)}, u32[]{:S(2)}, u32[]{:S(2)}) collective-permute-start(bf16[3,32,7168]{2,1,0:T(8,128)(2,1)} %get-tuple-element.17), channel_id=1, source_target_pairs={{0,96},{32,0},{64,32},{96,64},{1,97},{33,1},{65,33},{97,65},{2,98}... | collective-permute-start | bytes 4128776 | tf_op jit(solution)/shard_map/ppermute | solution.py:46
  186.6 7.5 %copy-start.9 = (f32[7168]{0:T(1024)S(1)}, f32[7168]{0:T(1024)}, u32[]{:S(2)}) copy-start(f32[7168]{0:T(1024)} %param.13) | copy-start | bytes 86020
  186.6 36.7 %copy-start.10 = (f32[7168]{0:T(1024)S(1)}, f32[7168]{0:T(1024)}, u32[]{:S(2)}) copy-start(f32[7168]{0:T(1024)} %param.19) | copy-start | bytes 86020
  186.6 34.4 %all-to-all-start.1 = ((bf16[3,32,7168]{2,0,1:T(4,128)(2,1)}), bf16[3,32,7168]{2,0,1:T(4,128)(2,1)S(1)}, u32[]{:S(2)}, u32[]{:S(2)}) async-start(bf16[3,32,7168]{2,0,1:T(4,128)(2,1)} %copy.139), calls=%async_computation.1 | async-start | bytes 3670016 | tf_op jit(solution)/shard_map/all_to_all | solution.py:112
  194.0 30.2 %copy-start.3 = (bf16[256,4,512]{2,1,0:T(4,128)(2,1)S(1)}, bf16[256,4,512]{2,1,0:T(4,128)(2,1)}, u32[]{:S(2)}) copy-start(bf16[256,4,512]{2,1,0:T(4,128)(2,1)} %param.21) | copy-start | bytes 3145732
  194.0 30.8 %copy-start.12 = (s32[256,4]{0,1:T(4,128)S(1)}, s32[256,4]{0,1:T(4,128)}, u32[]{:S(2)}) copy-start(s32[256,4]{0,1:T(4,128)} %param.22) | copy-start | bytes 12292
  194.0 127.3 %all-gather.11.cloned.1.call-start = ((), (), s32[]{:S(2)}) async-start(), calls=%async_computation.3 | async-start | bytes 29589504 | tf_op jit(solution)/shard_map/all_gather | solution.py:120
  223.3 9.1 %copy-start.11 = (s32[256]{0:T(256)S(1)}, s32[256]{0:T(256)}, u32[]{:S(2)}) copy-start(s32[256]{0:T(256)} %param.23) | copy-start | bytes 3076
  421.1 2.1 copy-start.4
  429.5 1.3 copy-start.8
  429.5 37.1 %copy-start.1 = (bf16[7168,32]{0,1:T(8,128)(2,1)S(1)}, bf16[7168,32]{0,1:T(8,128)(2,1)}, u32[]{:S(2)}) copy-start(bf16[7168,32]{0,1:T(8,128)(2,1)} %param.14) | copy-start | bytes 1376260
  430.0 0.8 copy-start.5
  430.8 34.7 %copy-start.6 = (f32[256,512]{1,0:T(8,128)S(1)}, f32[256,512]{1,0:T(8,128)}, u32[]{:S(2)}) copy-start(f32[256,512]{1,0:T(8,128)} %fusion.24) | copy-start | bytes 1572868
Sparse Core Ops, SparseCore 0:
  47.7 56.8 all-gather.8
  224.3 96.9 all-gather.10

commit v3 on v0

--- a/solution.py
+++ b/solution.py
@@ -116,19 +116,29 @@
     )
     mixed_rows = resid_in + moe_sum
     final_normed = rms_norm(mixed_rows, head_gain).astype(jnp.bfloat16)
-    gathered = lax.all_gather(final_normed, ALL_AXES, axis=1, tiled=False)
-    logits = jnp.einsum("tgd,wd->tgw", gathered, head, preferred_element_type=jnp.float32)
+    padded = -(-rows_dev // 16) * 16
+    block = jnp.concatenate(
+        [final_normed, jnp.zeros((padded - rows_dev, model_width), final_normed.dtype)]
+    )
+    gathered = lax.all_gather(block, ALL_AXES, axis=0, tiled=True)
+    devices = gathered.shape[0] // padded
+    logits = lax.dot_general(
+        gathered, head, (((1,), (1,)), ((), ())), preferred_element_type=jnp.float32
+    )
+    target_logits = logits.reshape(devices, padded, local_vocab)
     halves = rows_dev // slot_total
-    target_logits = logits.reshape(halves, slot_total, -1, local_vocab)
 
     def to_requests(values):
-        return jnp.transpose(values, (2, 0, 1)).reshape(requests, slot_total)
-
-    def from_requests(values):
-        return jnp.transpose(values.reshape(-1, halves, slot_total), (1, 2, 0))
+        return values[:, :rows_dev].reshape(requests, slot_total)
+
+    def from_requests(values, fill):
+        grid = values.reshape(devices, rows_dev)
+        return jnp.concatenate(
+            [grid, jnp.full((devices, padded - rows_dev), fill, grid.dtype)], axis=1
+        )
 
     ids_t = from_requests(
-        jnp.concatenate([local_ids, jnp.full((requests, 1), -1, jnp.int32)], axis=1)
+        jnp.concatenate([local_ids, jnp.full((requests, 1), -1, jnp.int32)], axis=1), -1
     )
     id_match_t = jnp.arange(local_vocab, dtype=jnp.int32) == ids_t[..., None]
     pick_target = to_requests(jnp.sum(jnp.where(id_match_t, target_logits, 0.0), axis=-1))
@@ -153,11 +163,17 @@
     position = (jnp.arange(slot_total, dtype=jnp.int32)[None, :] == reject_pos[:, None]).astype(
         jnp.float32
     )
-    weight_t = from_requests(position / sum_target)
-    target_at = jnp.sum(
-        weight_t[..., None] * jnp.exp(target_logits - from_requests(top_target)[..., None]), axis=1
-    )
-    target_at = jnp.transpose(target_at, (1, 0, 2)).reshape(requests, local_vocab)
+    weight_t = from_requests(position / sum_target, 0.0)
+    weighted = weight_t[..., None] * jnp.exp(
+        target_logits - from_requests(top_target, 0.0)[..., None]
+    )
+    target_at = jnp.stack(
+        [
+            jnp.sum(weighted[:, half * slot_total:(half + 1) * slot_total], axis=1)
+            for half in range(halves)
+        ],
+        axis=1,
+    ).reshape(requests, local_vocab)
     draft_at = jnp.sum(position[:, :DRAFTS, None] * draft_prob, axis=1)
     gap_rows = jnp.maximum(target_at - draft_at, 0.0)
     gap_total = gathered_sum(jnp.sum(gap_rows, axis=-1))

time: 463 us -> 443 us (0.957)
  local copies, waits for them, and re-layouts: 48.6 us -> 16.7 us
  matrix products: 29.5 us -> 35.7 us
  other arithmetic: 23.5 us -> 28.3 us
    unnamed x39 -> x31, local copies, waits for them, and re-layouts: 35.9 us -> 6.52 us
    dot_general x1, matrix products: 15.7 us -> 22.3 us  [body(): lax.dot_general(gathered, head, (((1,), (1,)), ((), ())), preferred_eleme...]
where the time goes in v3:
time: 443 us; the launch traced here: 441 us
  waiting for transfers between devices  230 us (52%)
  blocking collectives  103 us (23%)
  matrix products  35.7 us (8%)
  other arithmetic  28.3 us (6%)
  local copies, waits for them, and re-layouts  16.7 us (4%)
  between operations  14.6 us (3%)
  starting transfers between devices  12.6 us (3%)
    all_gather x1, waiting for transfers between devices, body(): gathered = lax.all_gather(block, ALL_AXES, axis=0, tiled=True)  88.3 us
    ppermute x3, waiting for transfers between devices, row_reduce_scatter(): total = total + lax.ppermute(chunk, 'row', pairs).astype(jnp.float32)  58.5 us
    all_gather x1, waiting for transfers between devices, body(): shard_piece = lax.all_gather(received, 'row', axis=1, tiled=True)  57 us
    all_gather x2, blocking collectives, merged_stats(): every = lax.all_gather(payload, axes, axis=0, tiled=False)  37.5 us
    all_to_all x1, blocking collectives, body(): lax.all_to_all(send_buffer, VOCAB_AXES, split_axis=1, concat_axis=1, tile...  33.8 us
    all_gather x2, blocking collectives, gathered_sum(): values = jnp.sum(lax.all_gather(values, axes, axis=0, tiled=False), axis=0)  31.7 us
    all_to_all x1, waiting for transfers between devices, body(): lax.all_to_all(summed, VOCAB_AXES, split_axis=1, concat_axis=1, tiled=True)  26.2 us
    dot_general x1, matrix products, body(): lax.dot_general(gathered, head, (((1,), (1,)), ((), ())), preferred_eleme...  22.3 us
  transfers between devices with their start and end apart: 6, of which 5 were waited for; matrix products, arithmetic and copies ran while one was open for 2% of the time, Pallas kernels for 0%

profile of v3, /device:TPU:0, one launch (start us, length us, event | category | flops | bytes accessed | tf_op | source)
XLA Modules:
  0.0 441.0 jit_solution(8807675585365552172)
XLA Ops:
  7.2 0.8 copy.109
  8.0 0.1 fusion.45
  8.2 1.1 fusion.30
  9.3 1.5 fusion
  10.8 1.2 copy.110
  12.0 33.8 %all_to_all.10 = bf16[3,32,7168]{2,0,1:T(4,128)(2,1)S(1)} all-to-all(bf16[3,32,7168]{2,0,1:T(4,128)(2,1)S(1)} %copy.110), channel_id=1, replica_groups=mesh['row'=4,'vz'=4,'vx'=4,'core'=2] {'vz','vx','core'}, dimensions={1} | all-to-all | bytes 2752512 | tf_op jit(solution)/shard_map/all_to_all | solution.py:102
  45.9 1.7 copy.111
  47.6 57.0 %all-gather.9.cloned.1.call-done = bf16[3,128,7168]{2,1,0:T(8,128)(2,1)} async-done(((bf16[3,32,7168]{2,1,0:T(8,128)(2,1)}), bf16[3,128,7168]{2,1,0:T(8,128)(2,1)}) %all-gather.9.cloned.1.call-update) | async-done | bytes 5505040 | tf_op jit(solution)/shard_map/all_gather | solution.py:103
  104.6 5.4 %fusion.5 = f32[384,256]{1,0:T(8,128)S(1)} fusion(bf16[384,7168]{1,0:T(8,128)(2,1)} %bitcast.117, bf16[1,7168,256]{2,1,0:T(8,128)(2,1)} %param.16), kind=kOutput, calls=%fused_computation.12 | convolution fusion | flops 1409286144 | bytes 9568256 | tf_op jit(solution)/shard_map/dot_general | solution.py:105
  110.0 0.9 copy-done.11
  110.9 1.6 fusion.21
  112.5 0.4 copy-done.4
  113.0 1.6 convolution_convert_fusion
  114.6 2.1 dynamic-slice_bitcast_fusion.2
  116.7 1.5 copy-done.2
  118.2 1.0 collective-permute-start
  119.2 1.5 collective-permute-start.1
  120.7 2.3 collective-permute-start.2
  123.1 57.8 %collective-permute-done = bf16[3,32,7168]{2,1,0:T(8,128)(2,1)S(1)} collective-permute-done((bf16[3,32,7168]{2,1,0:T(8,128)(2,1)}, bf16[3,32,7168]{2,1,0:T(8,128)(2,1)S(1)}, u32[]{:S(2)}, u32[]{:S(2)}) %collective-permute-start) | collective-permute-done | bytes 1376288 | tf_op jit(solution)/shard_map/ppermute | solution.py:46
  180.9 0.7 collective-permute-done.2
  181.6 2.6 fusion.9
  184.2 2.4 copy.113
  186.6 7.5 %all-to-all-start.1 = ((bf16[3,32,7168]{2,0,1:T(4,128)(2,1)}), bf16[3,32,7168]{2,0,1:T(4,128)(2,1)}, u32[]{:S(2)}, u32[]{:S(2)}) async-start(bf16[3,32,7168]{2,0,1:T(4,128)(2,1)} %copy.113), calls=%async_computation.1 | async-start | bytes 3670016 | tf_op jit(solution)/shard_map/all_to_all | solution.py:112
  194.1 0.2 all-gather.11.cloned.1.call-start
  194.4 0.4 select_reduce_fusion.1
  194.9 26.2 %all-to-all-done.1 = bf16[3,32,7168]{2,0,1:T(4,128)(2,1)} async-done(((bf16[3,32,7168]{2,0,1:T(4,128)(2,1)}), bf16[3,32,7168]{2,0,1:T(4,128)(2,1)}, u32[]{:S(2)}, u32[]{:S(2)}) %all-to-all-start.1) | async-done | bytes 1376288 | tf_op jit(solution)/shard_map/all_to_all | solution.py:112
  221.1 2.9 multiply_reduce_fusion
  224.0 0.1 multiply_convert_fusion
  224.1 0.7 concatenate.24
  224.9 0.5 reduce_max.45
  225.5 0.1 copy.135
  225.7 0.1 reshape.98
  225.9 7.0 %fusion.11 = (f32[256,4]{1,0:T(8,128)S(1)}, f32[256,4]{1,0:T(8,128)S(1)}) fusion(bf16[256,4,512]{2,1,0:T(4,128)(2,1)S(1)} %copy-done.3, f32[256,4]{1,0:T(8,128)S(1)} %reduce_max.46, s32[256,4]{1,0:T(8,128)S(1)} %copy.135), kind=kLoop, calls=%fused_computation.22 | loop fusion | flops 3143680 | bytes 1064960 | tf_op jit(solution)/shard_map/reduce_sum | solution.py:82
  233.0 0.1 copy.122
  233.1 0.1 fusion.42
  233.2 88.3 %all-gather.11.cloned.1.call-done = bf16[2048,7168]{1,0:T(8,128)(2,1)} async-done(((bf16[16,7168]{1,0:T(8,128)(2,1)}), bf16[2048,7168]{1,0:T(8,128)(2,1)}) %all-gather.11.cloned.1.call-update) | async-done | bytes 29360144 | tf_op jit(solution)/shard_map/all_gather | solution.py:123
  321.5 22.3 %fusion.59 = (f32[2048]{0:T(1024)S(1)}, f32[2048,512]{1,0:T(8,128)}) fusion(bf16[2048,7168]{1,0:T(8,128)(2,1)} %all-gather.11.cloned.1.call-done, bf16[512,7168]{1,0:T(8,128)(2,1)} %param.20), kind=kOutput, calls=%fused_computation.102 | convolution fusion | flops 15033432064 | bytes 40902656 | tf_op jit(solution)/shard_map/dot_general | solution.py:125
  343.9 3.2 exponential_reduce_fusion
  347.2 0.1 reshape.97
  347.3 0.1 reshape.96
  347.5 0.1 reduce_sum.164
  347.6 0.1 reshape.99
  347.8 24.3 %all-gather = f32[48,256,9]{1,2,0:T(8,128)S(1)} all-gather(f32[3,256,9]{1,2,0:T(8,128)S(1)} %pad_maximum_fusion.1), channel_id=2, replica_groups=mesh['row'=4,'vz'=4,'vx'=4,'core'=2] {'row','vz'}, dimensions={0}, use_global_device_ids=true | all-gather | bytes 470016 | tf_op jit(solution)/shard_map/all_gather | solution.py:26
  372.3 13.3 %all-gather.1 = f32[24,256,9]{1,2,0:T(8,128)S(1)} all-gather(f32[3,256,9]{1,2,0:T(8,128)S(1)} %copy.124), channel_id=3, replica_groups=mesh['row'=4,'vz'=4,'vx'=4,'core'=2] {'vx','core'}, dimensions={0}, use_global_device_ids=true | all-gather | bytes 248832 | tf_op jit(solution)/shard_map/all_gather | solution.py:26
  385.6 0.4 copy.133
  386.1 1.4 copy.132
  387.4 0.1 copy.137
  387.6 0.1 copy.138
  387.7 1.4 fusion.29
  389.2 0.1 slice_divide_fusion
  389.3 0.1 reshape.100
  389.5 2.6 exponential_multiply_fusion
  392.1 1.5 slice_reduce_fusion.1
  393.6 0.2 stack.41
  393.8 0.2 stack.42
  394.0 0.5 pad_maximum_fusion
  394.5 0.4 reshape.103
  394.8 0.1 fusion.41
  395.0 5.6 %fusion.16 = f32[256,512]{1,0:T(8,128)S(1)} fusion(bf16[256,4,512]{2,1,0:T(4,128)(2,1)S(1)} %copy-done.3, f32[256,4]{1,0:T(8,128)S(1)} %get-tuple-element.24, f32[256,4]{1,0:T(8,128)S(1)} %get-tuple-element.23, f32[256,4]{1,0:T(8,128)S(1)} %bitcast.109), kind=kLoop, calls=%fused_computation.30 | loop fusion | flops 2490368 | bytes 1585152 | tf_op jit(solution)/shard_map/reduce_sum | solution.py:177
  400.6 0.1 fusion.37
  400.7 22.3 %all-gather.4 = f32[16,1,256]{2,1,0:T(1,128)S(1)} all-gather(f32[1,1,256]{2,1,0:T(1,128)S(1)} %bitcast.115), channel_id=4, replica_groups=mesh['row'=4,'vz'=4,'vx'=4,'core'=2] {'row','vz'}, dimensions={0}, use_global_device_ids=true | all-gather | bytes 17408 | tf_op jit(solution)/shard_map/all_gather | solution.py:35
  423.1 9.3 %all-gather.5 = f32[8,1,256]{2,1,0:T(1,128)S(1)} all-gather(f32[1,1,256]{2,1,0:T(1,128)S(1)} %bitcast.116), channel_id=5, replica_groups=mesh['row'=4,'vz'=4,'vx'=4,'core'=2] {'vx','core'}, dimensions={0}, use_global_device_ids=true | all-gather | bytes 9216 | tf_op jit(solution)/shard_map/all_gather | solution.py:35
  432.5 1.0 divide_sqrt_fusion
  433.5 0.7 copy.129
  (62 shorter events, 1.4 us)
Async XLA Ops:
  7.2 187.2 %copy-start = (bf16[7168,32]{0,1:T(8,128)(2,1)S(1)}, bf16[7168,32]{0,1:T(8,128)(2,1)}, u32[]{:S(2)}) copy-start(bf16[7168,32]{0,1:T(8,128)(2,1)} %param.14) | copy-start | bytes 1376260
  7.2 97.4 %all-gather.9.cloned.1.call-start = ((), (), s32[]{:S(2)}) async-start(), calls=%async_computation.2 | async-start | bytes 6881280 | tf_op jit(solution)/shard_map/all_gather | solution.py:103
  104.6 5.4 %copy-start.10 = (bf16[3,128,7168]{2,1,0:T(8,128)(2,1)S(1)}, bf16[3,128,7168]{2,1,0:T(8,128)(2,1)}, u32[]{:S(2)}) copy-start(bf16[3,128,7168]{2,1,0:T(8,128)(2,1)} %all-gather.9.cloned.1.call-done) | copy-start | bytes 16515076
  104.6 6.3 %copy-start.11 = (bf16[1,7168,256]{2,1,0:T(8,128)(2,1)S(1)}, bf16[1,7168,256]{2,1,0:T(8,128)(2,1)}, u32[]{:S(2)}) copy-start(bf16[1,7168,256]{2,1,0:T(8,128)(2,1)} %param.17) | copy-start | bytes 11010052
  110.9 2.0 copy-start.4
  114.6 3.6 copy-start.2
  118.2 62.7 %collective-permute-start = (bf16[3,32,7168]{2,1,0:T(8,128)(2,1)}, bf16[3,32,7168]{2,1,0:T(8,128)(2,1)S(1)}, u32[]{:S(2)}, u32[]{:S(2)}) collective-permute-start(bf16[3,32,7168]{2,1,0:T(8,128)(2,1)} %get-tuple-element.16), channel_id=1, source_target_pairs={{0,32},{32,64},{64,96},{96,0},{1,33},{33,65},{65,97},{97,1},{2,34}... | collective-permute-start | bytes 4128776 | tf_op jit(solution)/shard_map/ppermute | solution.py:46
  119.2 61.6 %collective-permute-start.1 = (bf16[3,32,7168]{2,1,0:T(8,128)(2,1)}, bf16[3,32,7168]{2,1,0:T(8,128)(2,1)S(1)}, u32[]{:S(2)}, u32[]{:S(2)}) collective-permute-start(bf16[3,32,7168]{2,1,0:T(8,128)(2,1)} %get-tuple-element.18), channel_id=1, source_target_pairs={{0,64},{32,96},{64,0},{96,32},{1,65},{33,97},{65,1},{97,33},{2,66}... | collective-permute-start | bytes 4128776 | tf_op jit(solution)/shard_map/ppermute | solution.py:46
  120.7 60.8 %collective-permute-start.2 = (bf16[3,32,7168]{2,1,0:T(8,128)(2,1)}, bf16[3,32,7168]{2,1,0:T(8,128)(2,1)}, u32[]{:S(2)}, u32[]{:S(2)}) collective-permute-start(bf16[3,32,7168]{2,1,0:T(8,128)(2,1)} %get-tuple-element.17), channel_id=1, source_target_pairs={{0,96},{32,0},{64,32},{96,64},{1,97},{33,1},{65,33},{97,65},{2,98}... | collective-permute-start | bytes 4128776 | tf_op jit(solution)/shard_map/ppermute | solution.py:46
  184.2 10.2 %copy-start.5 = (bf16[10,7168]{1,0:T(8,128)(2,1)S(1)}, bf16[10,7168]{1,0:T(8,128)(2,1)}, u32[]{:S(2)}) copy-start(bf16[10,7168]{1,0:T(8,128)(2,1)} %param.12) | copy-start | bytes 430084
  184.2 10.2 %copy-start.6 = (f32[7168]{0:T(1024)S(1)}, f32[7168]{0:T(1024)}, u32[]{:S(2)}) copy-start(f32[7168]{0:T(1024)} %param.13) | copy-start | bytes 86020
  186.6 37.4 %copy-start.7 = (f32[7168]{0:T(1024)S(1)}, f32[7168]{0:T(1024)}, u32[]{:S(2)}) copy-start(f32[7168]{0:T(1024)} %param.19) | copy-start | bytes 86020
  186.6 34.5 %all-to-all-start.1 = ((bf16[3,32,7168]{2,0,1:T(4,128)(2,1)}), bf16[3,32,7168]{2,0,1:T(4,128)(2,1)}, u32[]{:S(2)}, u32[]{:S(2)}) async-start(bf16[3,32,7168]{2,0,1:T(4,128)(2,1)} %copy.113), calls=%async_computation.1 | async-start | bytes 3670016 | tf_op jit(solution)/shard_map/all_to_all | solution.py:112
  194.1 30.8 %copy-start.3 = (bf16[256,4,512]{2,1,0:T(4,128)(2,1)S(1)}, bf16[256,4,512]{2,1,0:T(4,128)(2,1)}, u32[]{:S(2)}) copy-start(bf16[256,4,512]{2,1,0:T(4,128)(2,1)} %param.21) | copy-start | bytes 3145732
  194.1 31.4 %copy-start.9 = (s32[256,4]{0,1:T(4,128)S(1)}, s32[256,4]{0,1:T(4,128)}, u32[]{:S(2)}) copy-start(s32[256,4]{0,1:T(4,128)} %param.22) | copy-start | bytes 12292
  194.1 127.4 %all-gather.11.cloned.1.call-start = ((), (), s32[]{:S(2)}) async-start(), calls=%async_computation.3 | async-start | bytes 29589504 | tf_op jit(solution)/shard_map/all_gather | solution.py:123
  224.0 9.1 %copy-start.8 = (s32[256]{0:T(256)S(1)}, s32[256]{0:T(256)}, u32[]{:S(2)}) copy-start(s32[256]{0:T(256)} %param.23) | copy-start | bytes 3076
  394.4 39.7 %copy-start.1 = (bf16[7168,32]{0,1:T(8,128)(2,1)S(1)}, bf16[7168,32]{0,1:T(8,128)(2,1)}, u32[]{:S(2)}) copy-start(bf16[7168,32]{0,1:T(8,128)(2,1)} %param.14) | copy-start | bytes 1376260
Sparse Core Ops, SparseCore 0:
  47.7 56.8 all-gather.8
  225.0 96.4 all-gather.10

commit v4 on v3

--- a/solution.py
+++ b/solution.py
@@ -21,13 +21,13 @@
 
 
 def merged_stats(top, total, pick):
-    payload = jnp.stack([top, total, pick])
+    payload = jnp.stack([top.T, total.T, pick.T])
     for axes in gather_groups():
         every = lax.all_gather(payload, axes, axis=0, tiled=False)
         best = jnp.max(every[:, 0], axis=0)
         scaled = jnp.sum(every[:, 1] * jnp.exp(every[:, 0] - best[None]), axis=0)
         payload = jnp.stack([best, scaled, jnp.sum(every[:, 2], axis=0)])
-    return payload[0], payload[1], payload[2]
+    return payload[0].T, payload[1].T, payload[2].T
 
 
 def gathered_sum(values):

time: 443 us -> 443 us (level)
  no operation moved by 1% of the time
where the time goes in v4:
time: 443 us; the launch traced here: 441 us
  waiting for transfers between devices  230 us (52%)
  blocking collectives  103 us (23%)
  matrix products  35.7 us (8%)
  other arithmetic  28.3 us (6%)
  local copies, waits for them, and re-layouts  16.6 us (4%)
  between operations  14.6 us (3%)
  starting transfers between devices  12.6 us (3%)
    all_gather x1, waiting for transfers between devices, body(): gathered = lax.all_gather(block, ALL_AXES, axis=0, tiled=True)  88.3 us
    ppermute x3, waiting for transfers between devices, row_reduce_scatter(): total = total + lax.ppermute(chunk, 'row', pairs).astype(jnp.float32)  58.5 us
    all_gather x1, waiting for transfers between devices, body(): shard_piece = lax.all_gather(received, 'row', axis=1, tiled=True)  57 us
    all_gather x2, blocking collectives, merged_stats(): every = lax.all_gather(payload, axes, axis=0, tiled=False)  37.5 us
    all_to_all x1, blocking collectives, body(): lax.all_to_all(send_buffer, VOCAB_AXES, split_axis=1, concat_axis=1, tile...  33.8 us
    all_gather x2, blocking collectives, gathered_sum(): values = jnp.sum(lax.all_gather(values, axes, axis=0, tiled=False), axis=0)  31.7 us
    all_to_all x1, waiting for transfers between devices, body(): lax.all_to_all(summed, VOCAB_AXES, split_axis=1, concat_axis=1, tiled=True)  26.2 us
    dot_general x1, matrix products, body(): lax.dot_general(gathered, head, (((1,), (1,)), ((), ())), preferred_eleme...  22.3 us
  transfers between devices with their start and end apart: 6, of which 5 were waited for; matrix products, arithmetic and copies ran while one was open for 2% of the time, Pallas kernels for 0%

profile of v4, /device:TPU:0, one launch (start us, length us, event | category | flops | bytes accessed | tf_op | source)
XLA Modules:
  0.0 440.9 jit_solution(7744941291380523766)
XLA Ops:
  7.2 0.8 copy.109
  8.0 0.1 fusion.46
  8.2 1.1 fusion.30
  9.3 1.5 fusion
  10.8 1.2 copy.110
  12.0 33.8 %all_to_all.10 = bf16[3,32,7168]{2,0,1:T(4,128)(2,1)S(1)} all-to-all(bf16[3,32,7168]{2,0,1:T(4,128)(2,1)S(1)} %copy.110), channel_id=1, replica_groups=mesh['row'=4,'vz'=4,'vx'=4,'core'=2] {'vz','vx','core'}, dimensions={1} | all-to-all | bytes 2752512 | tf_op jit(solution)/shard_map/all_to_all | solution.py:102
  45.9 1.7 copy.111
  47.6 57.0 %all-gather.9.cloned.1.call-done = bf16[3,128,7168]{2,1,0:T(8,128)(2,1)} async-done(((bf16[3,32,7168]{2,1,0:T(8,128)(2,1)}), bf16[3,128,7168]{2,1,0:T(8,128)(2,1)}) %all-gather.9.cloned.1.call-update) | async-done | bytes 5505040 | tf_op jit(solution)/shard_map/all_gather | solution.py:103
  104.6 5.4 %fusion.5 = f32[384,256]{1,0:T(8,128)S(1)} fusion(bf16[384,7168]{1,0:T(8,128)(2,1)} %bitcast.124, bf16[1,7168,256]{2,1,0:T(8,128)(2,1)} %param.16), kind=kOutput, calls=%fused_computation.12 | convolution fusion | flops 1409286144 | bytes 9568256 | tf_op jit(solution)/shard_map/dot_general | solution.py:105
  110.0 0.9 copy-done.11
  110.9 1.6 fusion.21
  112.5 0.4 copy-done.4
  113.0 1.6 convolution_convert_fusion
  114.6 2.1 dynamic-slice_bitcast_fusion.2
  116.7 1.5 copy-done.2
  118.2 1.0 collective-permute-start
  119.2 1.5 collective-permute-start.1
  120.7 2.3 collective-permute-start.2
  123.1 57.8 %collective-permute-done = bf16[3,32,7168]{2,1,0:T(8,128)(2,1)S(1)} collective-permute-done((bf16[3,32,7168]{2,1,0:T(8,128)(2,1)}, bf16[3,32,7168]{2,1,0:T(8,128)(2,1)S(1)}, u32[]{:S(2)}, u32[]{:S(2)}) %collective-permute-start) | collective-permute-done | bytes 1376288 | tf_op jit(solution)/shard_map/ppermute | solution.py:46
  180.9 0.7 collective-permute-done.2
  181.6 2.6 fusion.9
  184.2 2.4 copy.113
  186.6 7.5 %all-to-all-start.1 = ((bf16[3,32,7168]{2,0,1:T(4,128)(2,1)}), bf16[3,32,7168]{2,0,1:T(4,128)(2,1)}, u32[]{:S(2)}, u32[]{:S(2)}) async-start(bf16[3,32,7168]{2,0,1:T(4,128)(2,1)} %copy.113), calls=%async_computation.1 | async-start | bytes 3670016 | tf_op jit(solution)/shard_map/all_to_all | solution.py:112
  194.1 0.2 all-gather.11.cloned.1.call-start
  194.4 0.4 select_reduce_fusion.1
  194.9 26.2 %all-to-all-done.1 = bf16[3,32,7168]{2,0,1:T(4,128)(2,1)} async-done(((bf16[3,32,7168]{2,0,1:T(4,128)(2,1)}), bf16[3,32,7168]{2,0,1:T(4,128)(2,1)}, u32[]{:S(2)}, u32[]{:S(2)}) %all-to-all-start.1) | async-done | bytes 1376288 | tf_op jit(solution)/shard_map/all_to_all | solution.py:112
  221.1 2.9 multiply_reduce_fusion
  224.0 0.1 multiply_convert_fusion
  224.1 0.7 concatenate.24
  224.9 0.5 reduce_max.45
  225.5 0.1 copy.135
  225.7 0.1 reshape.98
  225.9 7.0 %fusion.11 = (f32[256,4]{1,0:T(8,128)S(1)}, f32[256,4]{1,0:T(8,128)S(1)}) fusion(bf16[256,4,512]{2,1,0:T(4,128)(2,1)S(1)} %copy-done.3, f32[256,4]{1,0:T(8,128)S(1)} %reduce_max.46, s32[256,4]{1,0:T(8,128)S(1)} %copy.135), kind=kLoop, calls=%fused_computation.22 | loop fusion | flops 3143680 | bytes 1064960 | tf_op jit(solution)/shard_map/reduce_sum | solution.py:82
  233.0 0.1 copy.122
  233.1 0.1 fusion.43
  233.2 88.3 %all-gather.11.cloned.1.call-done = bf16[2048,7168]{1,0:T(8,128)(2,1)} async-done(((bf16[16,7168]{1,0:T(8,128)(2,1)}), bf16[2048,7168]{1,0:T(8,128)(2,1)}) %all-gather.11.cloned.1.call-update) | async-done | bytes 29360144 | tf_op jit(solution)/shard_map/all_gather | solution.py:123
  321.5 22.3 %fusion.59 = (f32[2048]{0:T(1024)S(1)}, f32[2048,512]{1,0:T(8,128)}) fusion(bf16[2048,7168]{1,0:T(8,128)(2,1)} %all-gather.11.cloned.1.call-done, bf16[512,7168]{1,0:T(8,128)(2,1)} %param.20), kind=kOutput, calls=%fused_computation.103 | convolution fusion | flops 15033432064 | bytes 40902656 | tf_op jit(solution)/shard_map/dot_general | solution.py:125
  343.9 3.2 exponential_reduce_fusion
  347.2 0.1 reshape.97
  347.3 0.1 reshape.96
  347.5 0.1 reduce_sum.164
  347.6 0.1 reshape.99
  347.8 24.3 %all-gather = f32[48,9,256]{2,1,0:T(8,128)S(1)} all-gather(f32[3,9,256]{2,1,0:T(8,128)S(1)} %pad_maximum_fusion.1), channel_id=2, replica_groups=mesh['row'=4,'vz'=4,'vx'=4,'core'=2] {'row','vz'}, dimensions={0}, use_global_device_ids=true | all-gather | bytes 470016 | tf_op jit(solution)/shard_map/all_gather | solution.py:26
  372.3 13.3 %all-gather.1 = f32[24,9,256]{2,1,0:T(8,128)S(1)} all-gather(f32[3,9,256]{2,1,0:T(8,128)S(1)} %copy.124), channel_id=3, replica_groups=mesh['row'=4,'vz'=4,'vx'=4,'core'=2] {'vx','core'}, dimensions={0}, use_global_device_ids=true | all-gather | bytes 248832 | tf_op jit(solution)/shard_map/all_gather | solution.py:26
  385.6 0.4 copy.133
  386.1 1.4 copy.132
  387.4 0.1 copy.136
  387.5 1.4 fusion.29
  389.0 0.1 slice_divide_fusion
  389.1 0.1 reshape.100
  389.2 0.2 fusion.41
  389.4 0.1 reshape.102
  389.5 2.6 exponential_multiply_fusion
  392.1 1.5 slice_reduce_fusion.1
  393.6 0.2 stack.41
  393.7 0.2 stack.42
  394.0 0.5 pad_maximum_fusion
  394.4 0.4 reshape.103
  394.8 5.6 %fusion.16 = f32[256,512]{1,0:T(8,128)S(1)} fusion(bf16[256,4,512]{2,1,0:T(4,128)(2,1)S(1)} %copy-done.3, f32[256,4]{1,0:T(8,128)S(1)} %get-tuple-element.24, f32[256,4]{1,0:T(8,128)S(1)} %get-tuple-element.23, f32[256,4]{1,0:T(8,128)S(1)} %bitcast.116), kind=kLoop, calls=%fused_computation.30 | loop fusion | flops 2490368 | bytes 1585152 | tf_op jit(solution)/shard_map/reduce_sum | solution.py:177
  400.4 0.1 fusion.37
  400.6 22.3 %all-gather.4 = f32[16,1,256]{2,1,0:T(1,128)S(1)} all-gather(f32[1,1,256]{2,1,0:T(1,128)S(1)} %bitcast.122), channel_id=4, replica_groups=mesh['row'=4,'vz'=4,'vx'=4,'core'=2] {'row','vz'}, dimensions={0}, use_global_device_ids=true | all-gather | bytes 17408 | tf_op jit(solution)/shard_map/all_gather | solution.py:35
  422.9 9.3 %all-gather.5 = f32[8,1,256]{2,1,0:T(1,128)S(1)} all-gather(f32[1,1,256]{2,1,0:T(1,128)S(1)} %bitcast.123), channel_id=5, replica_groups=mesh['row'=4,'vz'=4,'vx'=4,'core'=2] {'vx','core'}, dimensions={0}, use_global_device_ids=true | all-gather | bytes 9216 | tf_op jit(solution)/shard_map/all_gather | solution.py:35
  432.3 1.0 divide_sqrt_fusion
  433.3 0.7 copy.129
  (60 shorter events, 1.3 us)
Async XLA Ops:
  7.2 187.2 %copy-start = (bf16[7168,32]{0,1:T(8,128)(2,1)S(1)}, bf16[7168,32]{0,1:T(8,128)(2,1)}, u32[]{:S(2)}) copy-start(bf16[7168,32]{0,1:T(8,128)(2,1)} %param.14) | copy-start | bytes 1376260
  7.2 97.4 %all-gather.9.cloned.1.call-start = ((), (), s32[]{:S(2)}) async-start(), calls=%async_computation.2 | async-start | bytes 6881280 | tf_op jit(solution)/shard_map/all_gather | solution.py:103
  104.6 5.4 %copy-start.10 = (bf16[3,128,7168]{2,1,0:T(8,128)(2,1)S(1)}, bf16[3,128,7168]{2,1,0:T(8,128)(2,1)}, u32[]{:S(2)}) copy-start(bf16[3,128,7168]{2,1,0:T(8,128)(2,1)} %all-gather.9.cloned.1.call-done) | copy-start | bytes 16515076
  104.6 6.3 %copy-start.11 = (bf16[1,7168,256]{2,1,0:T(8,128)(2,1)S(1)}, bf16[1,7168,256]{2,1,0:T(8,128)(2,1)}, u32[]{:S(2)}) copy-start(bf16[1,7168,256]{2,1,0:T(8,128)(2,1)} %param.17) | copy-start | bytes 11010052
  110.9 2.0 copy-start.4
  114.6 3.6 copy-start.2
  118.2 62.7 %collective-permute-start = (bf16[3,32,7168]{2,1,0:T(8,128)(2,1)}, bf16[3,32,7168]{2,1,0:T(8,128)(2,1)S(1)}, u32[]{:S(2)}, u32[]{:S(2)}) collective-permute-start(bf16[3,32,7168]{2,1,0:T(8,128)(2,1)} %get-tuple-element.16), channel_id=1, source_target_pairs={{0,32},{32,64},{64,96},{96,0},{1,33},{33,65},{65,97},{97,1},{2,34}... | collective-permute-start | bytes 4128776 | tf_op jit(solution)/shard_map/ppermute | solution.py:46
  119.2 61.6 %collective-permute-start.1 = (bf16[3,32,7168]{2,1,0:T(8,128)(2,1)}, bf16[3,32,7168]{2,1,0:T(8,128)(2,1)S(1)}, u32[]{:S(2)}, u32[]{:S(2)}) collective-permute-start(bf16[3,32,7168]{2,1,0:T(8,128)(2,1)} %get-tuple-element.18), channel_id=1, source_target_pairs={{0,64},{32,96},{64,0},{96,32},{1,65},{33,97},{65,1},{97,33},{2,66}... | collective-permute-start | bytes 4128776 | tf_op jit(solution)/shard_map/ppermute | solution.py:46
  120.7 60.8 %collective-permute-start.2 = (bf16[3,32,7168]{2,1,0:T(8,128)(2,1)}, bf16[3,32,7168]{2,1,0:T(8,128)(2,1)}, u32[]{:S(2)}, u32[]{:S(2)}) collective-permute-start(bf16[3,32,7168]{2,1,0:T(8,128)(2,1)} %get-tuple-element.17), channel_id=1, source_target_pairs={{0,96},{32,0},{64,32},{96,64},{1,97},{33,1},{65,33},{97,65},{2,98}... | collective-permute-start | bytes 4128776 | tf_op jit(solution)/shard_map/ppermute | solution.py:46
  184.2 10.2 %copy-start.5 = (bf16[10,7168]{1,0:T(8,128)(2,1)S(1)}, bf16[10,7168]{1,0:T(8,128)(2,1)}, u32[]{:S(2)}) copy-start(bf16[10,7168]{1,0:T(8,128)(2,1)} %param.12) | copy-start | bytes 430084
  184.2 10.2 %copy-start.6 = (f32[7168]{0:T(1024)S(1)}, f32[7168]{0:T(1024)}, u32[]{:S(2)}) copy-start(f32[7168]{0:T(1024)} %param.13) | copy-start | bytes 86020
  186.6 37.4 %copy-start.7 = (f32[7168]{0:T(1024)S(1)}, f32[7168]{0:T(1024)}, u32[]{:S(2)}) copy-start(f32[7168]{0:T(1024)} %param.19) | copy-start | bytes 86020
  186.6 34.5 %all-to-all-start.1 = ((bf16[3,32,7168]{2,0,1:T(4,128)(2,1)}), bf16[3,32,7168]{2,0,1:T(4,128)(2,1)}, u32[]{:S(2)}, u32[]{:S(2)}) async-start(bf16[3,32,7168]{2,0,1:T(4,128)(2,1)} %copy.113), calls=%async_computation.1 | async-start | bytes 3670016 | tf_op jit(solution)/shard_map/all_to_all | solution.py:112
  194.1 30.8 %copy-start.3 = (bf16[256,4,512]{2,1,0:T(4,128)(2,1)S(1)}, bf16[256,4,512]{2,1,0:T(4,128)(2,1)}, u32[]{:S(2)}) copy-start(bf16[256,4,512]{2,1,0:T(4,128)(2,1)} %param.21) | copy-start | bytes 3145732
  194.1 31.4 %copy-start.9 = (s32[256,4]{0,1:T(4,128)S(1)}, s32[256,4]{0,1:T(4,128)}, u32[]{:S(2)}) copy-start(s32[256,4]{0,1:T(4,128)} %param.22) | copy-start | bytes 12292
  194.1 127.4 %all-gather.11.cloned.1.call-start = ((), (), s32[]{:S(2)}) async-start(), calls=%async_computation.3 | async-start | bytes 29589504 | tf_op jit(solution)/shard_map/all_gather | solution.py:123
  224.0 9.1 %copy-start.8 = (s32[256]{0:T(256)S(1)}, s32[256]{0:T(256)}, u32[]{:S(2)}) copy-start(s32[256]{0:T(256)} %param.23) | copy-start | bytes 3076
  393.9 40.1 %copy-start.1 = (bf16[7168,32]{0,1:T(8,128)(2,1)S(1)}, bf16[7168,32]{0,1:T(8,128)(2,1)}, u32[]{:S(2)}) copy-start(bf16[7168,32]{0,1:T(8,128)(2,1)} %param.14) | copy-start | bytes 1376260
Sparse Core Ops, SparseCore 0:
  47.7 56.8 all-gather.8
  225.0 96.4 all-gather.10

commit v5 on v3

--- a/solution.py
+++ b/solution.py
@@ -120,7 +120,10 @@
     block = jnp.concatenate(
         [final_normed, jnp.zeros((padded - rows_dev, model_width), final_normed.dtype)]
     )
-    gathered = lax.all_gather(block, ALL_AXES, axis=0, tiled=True)
+    gather_axes = ALL_AXES[::-1]
+    sizes = [lax.axis_size(axis) for axis in gather_axes]
+    back = tuple(range(len(sizes) - 1, -1, -1))
+    gathered = lax.all_gather(block, gather_axes, axis=0, tiled=True)
     devices = gathered.shape[0] // padded
     logits = lax.dot_general(
         gathered, head, (((1,), (1,)), ((), ())), preferred_element_type=jnp.float32
@@ -128,11 +131,23 @@
     target_logits = logits.reshape(devices, padded, local_vocab)
     halves = rows_dev // slot_total
 
+    def natural(values):
+        rest = values.shape[1:]
+        grid = values.reshape(tuple(sizes) + rest)
+        order = back + tuple(range(len(sizes), grid.ndim))
+        return jnp.transpose(grid, order).reshape(values.shape)
+
+    def gathered_order(values):
+        rest = values.shape[1:]
+        grid = values.reshape(tuple(sizes[::-1]) + rest)
+        order = back + tuple(range(len(sizes), grid.ndim))
+        return jnp.transpose(grid, order).reshape(values.shape)
+
     def to_requests(values):
-        return values[:, :rows_dev].reshape(requests, slot_total)
+        return natural(values[:, :rows_dev]).reshape(requests, slot_total)
 
     def from_requests(values, fill):
-        grid = values.reshape(devices, rows_dev)
+        grid = gathered_order(values.reshape(devices, rows_dev))
         return jnp.concatenate(
             [grid, jnp.full((devices, padded - rows_dev), fill, grid.dtype)], axis=1
         )
@@ -173,7 +188,8 @@
             for half in range(halves)
         ],
         axis=1,
-    ).reshape(requests, local_vocab)
+    )
+    target_at = natural(target_at).reshape(requests, local_vocab)
     draft_at = jnp.sum(position[:, :DRAFTS, None] * draft_prob, axis=1)
     gap_rows = jnp.maximum(target_at - draft_at, 0.0)
     gap_total = gathered_sum(jnp.sum(gap_rows, axis=-1))

time: 443 us -> 444 us (level)
  no operation moved by 1% of the time
where the time goes in v5:
time: 444 us; the launch traced here: 443 us
  waiting for transfers between devices  230 us (52%)
  blocking collectives  103 us (23%)
  matrix products  35.7 us (8%)
  other arithmetic  28.3 us (6%)
  local copies, waits for them, and re-layouts  18.2 us (4%)
  between operations  14.6 us (3%)
  starting transfers between devices  12.6 us (3%)
    all_gather x1, waiting for transfers between devices, body(): gathered = lax.all_gather(block, gather_axes, axis=0, tiled=True)  88.3 us
    ppermute x3, waiting for transfers between devices, row_reduce_scatter(): total = total + lax.ppermute(chunk, 'row', pairs).astype(jnp.float32)  58.5 us
    all_gather x1, waiting for transfers between devices, body(): shard_piece = lax.all_gather(received, 'row', axis=1, tiled=True)  57 us
    all_gather x2, blocking collectives, merged_stats(): every = lax.all_gather(payload, axes, axis=0, tiled=False)  37.5 us
    all_to_all x1, blocking collectives, body(): lax.all_to_all(send_buffer, VOCAB_AXES, split_axis=1, concat_axis=1, tile...  33.8 us
    all_gather x2, blocking collectives, gathered_sum(): values = jnp.sum(lax.all_gather(values, axes, axis=0, tiled=False), axis=0)  31.7 us
    all_to_all x1, waiting for transfers between devices, body(): lax.all_to_all(summed, VOCAB_AXES, split_axis=1, concat_axis=1, tiled=True)  26.2 us
    dot_general x1, matrix products, body(): lax.dot_general(gathered, head, (((1,), (1,)), ((), ())), preferred_eleme...  22.3 us
  transfers between devices with their start and end apart: 6, of which 5 were waited for; matrix products, arithmetic and copies ran while one was open for 2% of the time, Pallas kernels for 0%

profile of v5, /device:TPU:0, one launch (start us, length us, event | category | flops | bytes accessed | tf_op | source)
XLA Modules:
  0.0 442.6 jit_solution(6716020822679837633)
XLA Ops:
  7.2 0.8 copy.160
  8.2 1.1 fusion.32
  9.3 1.5 fusion
  10.8 1.2 copy.161
  12.0 33.8 %all_to_all.10 = bf16[3,32,7168]{2,0,1:T(4,128)(2,1)S(1)} all-to-all(bf16[3,32,7168]{2,0,1:T(4,128)(2,1)S(1)} %copy.161), channel_id=1, replica_groups=mesh['row'=4,'vz'=4,'vx'=4,'core'=2] {'vz','vx','core'}, dimensions={1} | all-to-all | bytes 2752512 | tf_op jit(solution)/shard_map/all_to_all | solution.py:102
  45.9 1.7 copy.162
  47.6 57.0 %all-gather.8.cloned.1.call-done = bf16[3,128,7168]{2,1,0:T(8,128)(2,1)} async-done(((bf16[3,32,7168]{2,1,0:T(8,128)(2,1)}), bf16[3,128,7168]{2,1,0:T(8,128)(2,1)}) %all-gather.8.cloned.1.call-update) | async-done | bytes 5505040 | tf_op jit(solution)/shard_map/all_gather | solution.py:103
  104.6 5.4 %fusion.5 = f32[384,256]{1,0:T(8,128)S(1)} fusion(bf16[384,7168]{1,0:T(8,128)(2,1)} %bitcast.142, bf16[1,7168,256]{2,1,0:T(8,128)(2,1)} %param.16), kind=kOutput, calls=%fused_computation.12 | convolution fusion | flops 1409286144 | bytes 9568256 | tf_op jit(solution)/shard_map/dot_general | solution.py:105
  110.0 0.9 copy-done.11
  110.9 1.6 fusion.21
  112.5 0.4 copy-done.4
  113.0 1.6 convolution_convert_fusion
  114.6 2.1 dynamic-slice_bitcast_fusion.2
  116.7 1.5 copy-done.2
  118.2 1.0 collective-permute-start
  119.2 1.5 collective-permute-start.1
  120.7 2.3 collective-permute-start.2
  123.1 57.8 %collective-permute-done = bf16[3,32,7168]{2,1,0:T(8,128)(2,1)S(1)} collective-permute-done((bf16[3,32,7168]{2,1,0:T(8,128)(2,1)}, bf16[3,32,7168]{2,1,0:T(8,128)(2,1)S(1)}, u32[]{:S(2)}, u32[]{:S(2)}) %collective-permute-start) | collective-permute-done | bytes 1376288 | tf_op jit(solution)/shard_map/ppermute | solution.py:46
  180.9 0.7 collective-permute-done.2
  181.6 2.6 fusion.9
  184.2 2.4 copy.164
  186.6 7.5 %all-to-all-start.1 = ((bf16[3,32,7168]{2,0,1:T(4,128)(2,1)}), bf16[3,32,7168]{2,0,1:T(4,128)(2,1)}, u32[]{:S(2)}, u32[]{:S(2)}) async-start(bf16[3,32,7168]{2,0,1:T(4,128)(2,1)} %copy.164), calls=%async_computation.1 | async-start | bytes 3670016 | tf_op jit(solution)/shard_map/all_to_all | solution.py:112
  194.1 0.2 all-gather.10.cloned.1.call-start
  194.4 0.4 select_reduce_fusion.1
  194.9 26.2 %all-to-all-done.1 = bf16[3,32,7168]{2,0,1:T(4,128)(2,1)} async-done(((bf16[3,32,7168]{2,0,1:T(4,128)(2,1)}), bf16[3,32,7168]{2,0,1:T(4,128)(2,1)}, u32[]{:S(2)}, u32[]{:S(2)}) %all-to-all-start.1) | async-done | bytes 1376288 | tf_op jit(solution)/shard_map/all_to_all | solution.py:112
  221.1 2.9 multiply_reduce_fusion
  224.0 0.1 multiply_convert_fusion
  224.1 0.7 concatenate.25
  224.9 0.5 reduce_max.45
  225.5 0.1 copy.195
  225.7 0.1 reshape_reshape.23
  225.9 7.0 %fusion.11 = (f32[256,4]{1,0:T(8,128)S(1)}, f32[256,4]{1,0:T(8,128)S(1)}) fusion(bf16[256,4,512]{2,1,0:T(4,128)(2,1)S(1)} %copy-done.3, f32[256,4]{1,0:T(8,128)S(1)} %reduce_max.46, s32[256,4]{1,0:T(8,128)S(1)} %copy.195), kind=kLoop, calls=%fused_computation.22 | loop fusion | flops 3143680 | bytes 1064960 | tf_op jit(solution)/shard_map/reduce_sum | solution.py:82
  233.1 0.1 fusion.43
  233.3 88.3 %all-gather.10.cloned.1.call-done = bf16[2048,7168]{1,0:T(8,128)(2,1)} async-done(((bf16[16,7168]{1,0:T(8,128)(2,1)}), bf16[2048,7168]{1,0:T(8,128)(2,1)}) %all-gather.10.cloned.1.call-update) | async-done | bytes 29360144 | tf_op jit(solution)/shard_map/all_gather | solution.py:126
  321.5 22.3 %fusion.60 = (f32[2048]{0:T(1024)S(1)}, f32[2048,512]{1,0:T(8,128)}) fusion(bf16[2048,7168]{1,0:T(8,128)(2,1)} %all-gather.10.cloned.1.call-done, bf16[512,7168]{1,0:T(8,128)(2,1)} %param.20), kind=kOutput, calls=%fused_computation.104 | convolution fusion | flops 15033432064 | bytes 40902656 | tf_op jit(solution)/shard_map/dot_general | solution.py:128
  343.9 3.2 exponential_reduce_fusion
  347.3 0.1 reshape_reshape.22
  347.5 0.1 reshape_reshape.21
  347.9 0.1 reshape_reshape.24
  348.2 24.3 %all-gather = f32[48,256,9]{1,2,0:T(8,128)S(1)} all-gather(f32[3,256,9]{1,2,0:T(8,128)S(1)} %pad_maximum_fusion), channel_id=2, replica_groups=mesh['row'=4,'vz'=4,'vx'=4,'core'=2] {'row','vz'}, dimensions={0}, use_global_device_ids=true | all-gather | bytes 470016 | tf_op jit(solution)/shard_map/all_gather | solution.py:26
  372.6 13.3 %all-gather.1 = f32[24,256,9]{1,2,0:T(8,128)S(1)} all-gather(f32[3,256,9]{1,2,0:T(8,128)S(1)} %copy.179), channel_id=3, replica_groups=mesh['row'=4,'vz'=4,'vx'=4,'core'=2] {'vx','core'}, dimensions={0}, use_global_device_ids=true | all-gather | bytes 248832 | tf_op jit(solution)/shard_map/all_gather | solution.py:26
  386.0 0.4 copy.193
  386.4 1.4 copy.192
  387.8 0.1 copy.197
  387.9 0.1 copy.198
  388.0 1.4 fusion.29
  389.5 0.1 slice_divide_fusion
  389.6 0.1 fusion.42
  389.8 5.6 %fusion.16 = f32[256,512]{1,0:T(8,128)S(1)} fusion(bf16[256,4,512]{2,1,0:T(4,128)(2,1)S(1)} %copy-done.3, f32[256,4]{1,0:T(8,128)S(1)} %get-tuple-element.24, f32[256,4]{1,0:T(8,128)S(1)} %get-tuple-element.23, f32[256,4]{1,0:T(8,128)S(1)} %bitcast.128), kind=kLoop, calls=%fused_computation.30 | loop fusion | flops 2490368 | bytes 1585152 | tf_op jit(solution)/shard_map/reduce_sum | solution.py:193
  395.4 0.3 reduce_sum.174
  395.7 0.1 reshape_reshape.25
  395.9 0.1 reshape_reshape.26
  396.1 2.6 exponential_multiply_fusion
  398.7 1.5 slice_reduce_fusion.1
  400.3 0.2 maximum_bitcast_fusion
  400.5 0.5 fusion.31
  401.0 0.3 copy.187
  401.3 0.2 reshape.100
  401.5 22.3 %all-gather.3 = f32[16,1,256]{2,1,0:T(1,128)S(1)} all-gather(f32[1,1,256]{2,1,0:T(1,128)S(1)} %reshape.100), channel_id=1, replica_groups=mesh['row'=4,'vz'=4,'vx'=4,'core'=2] {'row','vz'}, dimensions={0}, use_global_device_ids=true | all-gather | bytes 17408 | tf_op jit(solution)/shard_map/all_gather | solution.py:35
  423.9 9.3 %all-gather.4 = f32[8,1,256]{2,1,0:T(1,128)S(1)} all-gather(f32[1,1,256]{2,1,0:T(1,128)S(1)} %bitcast.141), channel_id=4, replica_groups=mesh['row'=4,'vz'=4,'vx'=4,'core'=2] {'vx','core'}, dimensions={0}, use_global_device_ids=true | all-gather | bytes 9216 | tf_op jit(solution)/shard_map/all_gather | solution.py:35
  433.2 0.4 copy.185
  433.6 0.4 reshape_reshape.27
  434.0 0.7 copy.189
  434.7 1.0 divide_sqrt_fusion
  (72 shorter events, 2.0 us)
Async XLA Ops:
  7.2 187.2 %copy-start = (bf16[7168,32]{0,1:T(8,128)(2,1)S(1)}, bf16[7168,32]{0,1:T(8,128)(2,1)}, u32[]{:S(2)}) copy-start(bf16[7168,32]{0,1:T(8,128)(2,1)} %param.14) | copy-start | bytes 1376260
  7.2 97.4 %all-gather.8.cloned.1.call-start = ((), (), s32[]{:S(2)}) async-start(), calls=%async_computation.2 | async-start | bytes 6881280 | tf_op jit(solution)/shard_map/all_gather | solution.py:103
  104.6 5.4 %copy-start.10 = (bf16[3,128,7168]{2,1,0:T(8,128)(2,1)S(1)}, bf16[3,128,7168]{2,1,0:T(8,128)(2,1)}, u32[]{:S(2)}) copy-start(bf16[3,128,7168]{2,1,0:T(8,128)(2,1)} %all-gather.8.cloned.1.call-done) | copy-start | bytes 16515076
  104.6 6.3 %copy-start.11 = (bf16[1,7168,256]{2,1,0:T(8,128)(2,1)S(1)}, bf16[1,7168,256]{2,1,0:T(8,128)(2,1)}, u32[]{:S(2)}) copy-start(bf16[1,7168,256]{2,1,0:T(8,128)(2,1)} %param.17) | copy-start | bytes 11010052
  110.9 2.0 copy-start.4
  114.6 3.6 copy-start.2
  118.2 62.7 %collective-permute-start = (bf16[3,32,7168]{2,1,0:T(8,128)(2,1)}, bf16[3,32,7168]{2,1,0:T(8,128)(2,1)S(1)}, u32[]{:S(2)}, u32[]{:S(2)}) collective-permute-start(bf16[3,32,7168]{2,1,0:T(8,128)(2,1)} %get-tuple-element.16), channel_id=1, source_target_pairs={{0,32},{32,64},{64,96},{96,0},{1,33},{33,65},{65,97},{97,1},{2,34}... | collective-permute-start | bytes 4128776 | tf_op jit(solution)/shard_map/ppermute | solution.py:46
  119.2 61.6 %collective-permute-start.1 = (bf16[3,32,7168]{2,1,0:T(8,128)(2,1)}, bf16[3,32,7168]{2,1,0:T(8,128)(2,1)S(1)}, u32[]{:S(2)}, u32[]{:S(2)}) collective-permute-start(bf16[3,32,7168]{2,1,0:T(8,128)(2,1)} %get-tuple-element.18), channel_id=1, source_target_pairs={{0,64},{32,96},{64,0},{96,32},{1,65},{33,97},{65,1},{97,33},{2,66}... | collective-permute-start | bytes 4128776 | tf_op jit(solution)/shard_map/ppermute | solution.py:46
  120.7 60.8 %collective-permute-start.2 = (bf16[3,32,7168]{2,1,0:T(8,128)(2,1)}, bf16[3,32,7168]{2,1,0:T(8,128)(2,1)}, u32[]{:S(2)}, u32[]{:S(2)}) collective-permute-start(bf16[3,32,7168]{2,1,0:T(8,128)(2,1)} %get-tuple-element.17), channel_id=1, source_target_pairs={{0,96},{32,0},{64,32},{96,64},{1,97},{33,1},{65,33},{97,65},{2,98}... | collective-permute-start | bytes 4128776 | tf_op jit(solution)/shard_map/ppermute | solution.py:46
  184.2 10.2 %copy-start.5 = (bf16[10,7168]{1,0:T(8,128)(2,1)S(1)}, bf16[10,7168]{1,0:T(8,128)(2,1)}, u32[]{:S(2)}) copy-start(bf16[10,7168]{1,0:T(8,128)(2,1)} %param.12) | copy-start | bytes 430084
  184.2 10.2 %copy-start.6 = (f32[7168]{0:T(1024)S(1)}, f32[7168]{0:T(1024)}, u32[]{:S(2)}) copy-start(f32[7168]{0:T(1024)} %param.13) | copy-start | bytes 86020
  186.6 37.4 %copy-start.7 = (f32[7168]{0:T(1024)S(1)}, f32[7168]{0:T(1024)}, u32[]{:S(2)}) copy-start(f32[7168]{0:T(1024)} %param.19) | copy-start | bytes 86020
  186.6 34.5 %all-to-all-start.1 = ((bf16[3,32,7168]{2,0,1:T(4,128)(2,1)}), bf16[3,32,7168]{2,0,1:T(4,128)(2,1)}, u32[]{:S(2)}, u32[]{:S(2)}) async-start(bf16[3,32,7168]{2,0,1:T(4,128)(2,1)} %copy.164), calls=%async_computation.1 | async-start | bytes 3670016 | tf_op jit(solution)/shard_map/all_to_all | solution.py:112
  194.1 30.8 %copy-start.3 = (bf16[256,4,512]{2,1,0:T(4,128)(2,1)S(1)}, bf16[256,4,512]{2,1,0:T(4,128)(2,1)}, u32[]{:S(2)}) copy-start(bf16[256,4,512]{2,1,0:T(4,128)(2,1)} %param.21) | copy-start | bytes 3145732
  194.1 31.4 %copy-start.9 = (s32[256,4]{0,1:T(4,128)S(1)}, s32[256,4]{0,1:T(4,128)}, u32[]{:S(2)}) copy-start(s32[256,4]{0,1:T(4,128)} %param.22) | copy-start | bytes 12292
  194.1 127.4 %all-gather.10.cloned.1.call-start = ((), (), s32[]{:S(2)}) async-start(), calls=%async_computation.3 | async-start | bytes 29589504 | tf_op jit(solution)/shard_map/all_gather | solution.py:126
  224.0 9.1 %copy-start.8 = (s32[256]{0:T(256)S(1)}, s32[256]{0:T(256)}, u32[]{:S(2)}) copy-start(s32[256]{0:T(256)} %param.23) | copy-start | bytes 3076
  400.3 35.4 %copy-start.1 = (bf16[7168,32]{0,1:T(8,128)(2,1)S(1)}, bf16[7168,32]{0,1:T(8,128)(2,1)}, u32[]{:S(2)}) copy-start(bf16[7168,32]{0,1:T(8,128)(2,1)} %param.14) | copy-start | bytes 1376260
Sparse Core Ops, SparseCore 0:
  47.7 56.8 all-gather.7
  225.0 96.4 all-gather.9

commit v6 on v3

--- a/solution.py
+++ b/solution.py
@@ -93,13 +93,21 @@
     earlier = jnp.cumsum(chosen_int, axis=0) - chosen_int
     slot_ids = jnp.arange(capacity, dtype=jnp.int32)[None, :, None]
     selector = ((earlier.T[:, None, :] == slot_ids) & chosen.T[:, None, :]).astype(jnp.float32)
+    per_expert = capacity * model_width
+    fold = 4 if per_expert % (4 * 128) == 0 else capacity
     send_buffer = jnp.einsum(
-        "esr,rd->sed", selector.astype(jnp.bfloat16), normed, preferred_element_type=jnp.float32
+        "esr,rd->esd", selector.astype(jnp.bfloat16), normed, preferred_element_type=jnp.float32
     ).astype(jnp.bfloat16)
     gate_w = w_gate[0]
     up_w = w_up[0]
     down_w = w_down[0]
-    received = lax.all_to_all(send_buffer, VOCAB_AXES, split_axis=1, concat_axis=1, tiled=True)
+
+    def exchange(buffer):
+        folded = buffer.reshape(buffer.shape[0], fold, per_expert // fold)
+        moved = lax.all_to_all(folded, VOCAB_AXES, split_axis=0, concat_axis=0, tiled=True)
+        return moved.reshape(buffer.shape)
+
+    received = jnp.transpose(exchange(send_buffer), (1, 0, 2))
     shard_piece = lax.all_gather(received, "row", axis=1, tiled=True)
     flat_rows = shard_piece.reshape(-1, model_width)
     gate_out = jnp.dot(flat_rows, gate_w, preferred_element_type=jnp.float32)
@@ -109,10 +117,10 @@
     summed = row_reduce_scatter(
         down_out.reshape(capacity, row_count, -1, model_width)
     )
-    returned = lax.all_to_all(summed, VOCAB_AXES, split_axis=1, concat_axis=1, tiled=True)
+    returned = exchange(jnp.transpose(summed, (1, 0, 2)))
     combine = selector * weights.T[:, None, :]
     moe_sum = jnp.einsum(
-        "esr,sed->rd", combine, returned.astype(jnp.float32), precision=lax.Precision.HIGHEST
+        "esr,esd->rd", combine, returned.astype(jnp.float32), precision=lax.Precision.HIGHEST
     )
     mixed_rows = resid_in + moe_sum
     final_normed = rms_norm(mixed_rows, head_gain).astype(jnp.bfloat16)

time: 443 us -> 444 us (level)
  local copies, waits for them, and re-layouts: 16.7 us -> 28.4 us
  waiting for transfers between devices: 230 us -> 225 us
  blocking collectives: 103 us -> 98.3 us
    reshape x0 -> x4, local copies, waits for them, and re-layouts: none -> 12.9 us  [the longest x2 7.84 us: exchange(): return moved.reshape(buffer.shape)]
    all_to_all x1, waiting for transfers between devices: 26.2 us -> 20.8 us  [exchange(): lax.all_to_all(folded, VOCAB_AXES, split_axis=0, concat_axis=0, tiled=True)]
    all_to_all x1, blocking collectives: 33.8 us -> 29.1 us  [exchange(): lax.all_to_all(folded, VOCAB_AXES, split_axis=0, concat_axis=0, tiled=True)]
where the time goes in v6:
time: 444 us; the launch traced here: 442 us
  waiting for transfers between devices  225 us (51%)
  blocking collectives  98.3 us (22%)
  matrix products  35.2 us (8%)
  local copies, waits for them, and re-layouts  28.4 us (6%)
  other arithmetic  28.3 us (6%)
  between operations  14.6 us (3%)
  starting transfers between devices  12.3 us (3%)
    all_gather x1, waiting for transfers between devices, body(): gathered = lax.all_gather(block, ALL_AXES, axis=0, tiled=True)  88.1 us
    ppermute x3, waiting for transfers between devices, row_reduce_scatter(): total = total + lax.ppermute(chunk, 'row', pairs).astype(jnp.float32)  58.5 us
    all_gather x1, waiting for transfers between devices, body(): shard_piece = lax.all_gather(received, 'row', axis=1, tiled=True)  57.2 us
    all_gather x2, blocking collectives, merged_stats(): every = lax.all_gather(payload, axes, axis=0, tiled=False)  37.6 us
    all_gather x2, blocking collectives, gathered_sum(): values = jnp.sum(lax.all_gather(values, axes, axis=0, tiled=False), axis=0)  31.7 us
    all_to_all x1, blocking collectives, exchange(): lax.all_to_all(folded, VOCAB_AXES, split_axis=0, concat_axis=0, tiled=True)  29.1 us
    dot_general x1, matrix products, body(): lax.dot_general(gathered, head, (((1,), (1,)), ((), ())), preferred_eleme...  22.3 us
    all_to_all x1, waiting for transfers between devices, exchange(): lax.all_to_all(folded, VOCAB_AXES, split_axis=0, concat_axis=0, tiled=True)  20.8 us
  transfers between devices with their start and end apart: 6, of which 5 were waited for; matrix products, arithmetic and copies ran while one was open for 2% of the time, Pallas kernels for 0%

profile of v6, /device:TPU:0, one launch (start us, length us, event | category | flops | bytes accessed | tf_op | source)
XLA Modules:
  0.0 441.6 jit_solution(4817299258733261007)
XLA Ops:
  7.2 0.8 copy.88
  8.0 0.1 fusion.45
  8.2 1.1 fusion.30
  9.3 1.5 convolution_convert_fusion.1
  10.8 1.2 copy.89
  12.0 2.5 reshape.106
  14.6 29.1 %all_to_all.10 = bf16[32,4,5376]{2,1,0:T(4,128)(2,1)} all-to-all(bf16[32,4,5376]{2,1,0:T(4,128)(2,1)} %reshape.106), channel_id=1, replica_groups=mesh['row'=4,'vz'=4,'vx'=4,'core'=2] {'vz','vx','core'}, dimensions={0} | all-to-all | bytes 2752512 | tf_op jit(solution)/shard_map/all_to_all | solution.py:107
  43.7 3.9 reshape.107
  47.6 1.7 copy.90
  49.3 57.2 %all-gather.9.cloned.1.call-done = bf16[3,128,7168]{2,1,0:T(8,128)(2,1)} async-done(((bf16[3,32,7168]{2,1,0:T(8,128)(2,1)}), bf16[3,128,7168]{2,1,0:T(8,128)(2,1)}) %all-gather.9.cloned.1.call-update) | async-done | bytes 5505040 | tf_op jit(solution)/shard_map/all_gather | solution.py:111
  106.5 5.4 %fusion.4 = f32[384,256]{1,0:T(8,128)S(1)} fusion(bf16[384,7168]{1,0:T(8,128)(2,1)} %bitcast.119, bf16[1,7168,256]{2,1,0:T(8,128)(2,1)} %param.16), kind=kOutput, calls=%fused_computation.11 | convolution fusion | flops 1409286144 | bytes 9568256 | tf_op jit(solution)/shard_map/dot_general | solution.py:113
  111.9 0.9 copy-done.11
  112.8 1.6 fusion.21
  114.4 0.4 copy-done.4
  114.9 1.6 convolution_convert_fusion
  116.5 2.1 dynamic-slice_bitcast_fusion.2
  118.6 1.5 copy-done.2
  120.1 1.0 collective-permute-start
  121.1 1.5 collective-permute-start.1
  122.6 2.3 collective-permute-start.2
  125.0 57.8 %collective-permute-done = bf16[3,32,7168]{2,1,0:T(8,128)(2,1)S(1)} collective-permute-done((bf16[3,32,7168]{2,1,0:T(8,128)(2,1)}, bf16[3,32,7168]{2,1,0:T(8,128)(2,1)S(1)}, u32[]{:S(2)}, u32[]{:S(2)}) %collective-permute-start) | collective-permute-done | bytes 1376288 | tf_op jit(solution)/shard_map/ppermute | solution.py:46
  182.8 0.7 collective-permute-done.2
  183.5 2.6 fusion.16
  186.1 1.2 copy.92
  187.3 2.5 reshape.110
  189.8 7.3 %all-to-all-start.1 = ((bf16[32,4,5376]{2,1,0:T(4,128)(2,1)}), bf16[32,4,5376]{2,1,0:T(4,128)(2,1)}, u32[]{:S(2)}, u32[]{:S(2)}) async-start(bf16[32,4,5376]{2,1,0:T(4,128)(2,1)} %reshape.110), calls=%async_computation.1 | async-start | bytes 2752512 | tf_op jit(solution)/shard_map/all_to_all | solution.py:107
  197.3 0.4 select_reduce_fusion.1
  197.8 20.8 %all-to-all-done.1 = bf16[32,4,5376]{2,1,0:T(4,128)(2,1)} async-done(((bf16[32,4,5376]{2,1,0:T(4,128)(2,1)}), bf16[32,4,5376]{2,1,0:T(4,128)(2,1)}, u32[]{:S(2)}, u32[]{:S(2)}) %all-to-all-start.1) | async-done | bytes 1376288 | tf_op jit(solution)/shard_map/all_to_all | solution.py:107
  218.6 3.9 reshape.111
  222.5 2.3 multiply_reduce_fusion
  224.8 0.1 multiply_convert_fusion
  225.0 0.7 concatenate.24
  225.7 0.5 reduce_max.45
  226.3 0.1 copy.114
  226.5 0.1 reshape.114
  226.7 7.0 %fusion.10 = (f32[256,4]{1,0:T(8,128)S(1)}, f32[256,4]{1,0:T(8,128)S(1)}) fusion(bf16[256,4,512]{2,1,0:T(4,128)(2,1)S(1)} %copy-done.3, f32[256,4]{1,0:T(8,128)S(1)} %reduce_max.46, s32[256,4]{1,0:T(8,128)S(1)} %copy.114), kind=kLoop, calls=%fused_computation.21 | loop fusion | flops 3143680 | bytes 1064960 | tf_op jit(solution)/shard_map/reduce_sum | solution.py:82
  233.8 0.1 copy.101
  233.9 0.1 fusion.42
  234.0 88.1 %all-gather.11.cloned.1.call-done = bf16[2048,7168]{1,0:T(8,128)(2,1)} async-done(((bf16[16,7168]{1,0:T(8,128)(2,1)}), bf16[2048,7168]{1,0:T(8,128)(2,1)}) %all-gather.11.cloned.1.call-update) | async-done | bytes 29360144 | tf_op jit(solution)/shard_map/all_gather | solution.py:131
  322.1 22.3 %fusion.59 = (f32[2048]{0:T(1024)S(1)}, f32[2048,512]{1,0:T(8,128)}) fusion(bf16[2048,7168]{1,0:T(8,128)(2,1)} %all-gather.11.cloned.1.call-done, bf16[512,7168]{1,0:T(8,128)(2,1)} %param.20), kind=kOutput, calls=%fused_computation.102 | convolution fusion | flops 15033432064 | bytes 40902656 | tf_op jit(solution)/shard_map/dot_general | solution.py:133
  344.5 3.2 exponential_reduce_fusion
  347.9 0.1 reshape.112
  348.1 0.1 reduce_sum.164
  348.4 24.5 %all-gather = f32[48,256,9]{1,2,0:T(8,128)S(1)} all-gather(f32[3,256,9]{1,2,0:T(8,128)S(1)} %pad_maximum_fusion.1), channel_id=2, replica_groups=mesh['row'=4,'vz'=4,'vx'=4,'core'=2] {'row','vz'}, dimensions={0}, use_global_device_ids=true | all-gather | bytes 470016 | tf_op jit(solution)/shard_map/all_gather | solution.py:26
  373.2 13.1 %all-gather.1 = f32[24,256,9]{1,2,0:T(8,128)S(1)} all-gather(f32[3,256,9]{1,2,0:T(8,128)S(1)} %copy.103), channel_id=3, replica_groups=mesh['row'=4,'vz'=4,'vx'=4,'core'=2] {'vx','core'}, dimensions={0}, use_global_device_ids=true | all-gather | bytes 248832 | tf_op jit(solution)/shard_map/all_gather | solution.py:26
  386.2 0.4 copy.112
  386.7 1.4 copy.111
  388.0 0.1 copy.116
  388.2 0.1 copy.117
  388.3 1.4 fusion.29
  389.8 0.1 slice_divide_fusion
  390.1 2.6 exponential_multiply_fusion
  392.7 1.5 slice_reduce_fusion.1
  394.2 0.2 stack.41
  394.4 0.2 stack.42
  394.6 0.5 pad_maximum_fusion
  395.1 0.4 reshape.119
  395.4 0.1 fusion.41
  395.6 5.6 %fusion.15 = f32[256,512]{1,0:T(8,128)S(1)} fusion(bf16[256,4,512]{2,1,0:T(4,128)(2,1)S(1)} %copy-done.3, f32[256,4]{1,0:T(8,128)S(1)} %get-tuple-element.22, f32[256,4]{1,0:T(8,128)S(1)} %get-tuple-element.21, f32[256,4]{1,0:T(8,128)S(1)} %bitcast.111), kind=kLoop, calls=%fused_computation.29 | loop fusion | flops 2490368 | bytes 1585152 | tf_op jit(solution)/shard_map/reduce_sum | solution.py:185
  401.2 0.1 fusion.37
  401.3 22.3 %all-gather.4 = f32[16,1,256]{2,1,0:T(1,128)S(1)} all-gather(f32[1,1,256]{2,1,0:T(1,128)S(1)} %bitcast.117), channel_id=4, replica_groups=mesh['row'=4,'vz'=4,'vx'=4,'core'=2] {'row','vz'}, dimensions={0}, use_global_device_ids=true | all-gather | bytes 17408 | tf_op jit(solution)/shard_map/all_gather | solution.py:35
  423.7 9.3 %all-gather.5 = f32[8,1,256]{2,1,0:T(1,128)S(1)} all-gather(f32[1,1,256]{2,1,0:T(1,128)S(1)} %bitcast.118), channel_id=5, replica_groups=mesh['row'=4,'vz'=4,'vx'=4,'core'=2] {'vx','core'}, dimensions={0}, use_global_device_ids=true | all-gather | bytes 9216 | tf_op jit(solution)/shard_map/all_gather | solution.py:35
  433.1 1.0 divide_sqrt_fusion
  434.1 0.7 copy.108
  (66 shorter events, 1.7 us)
Async XLA Ops:
  7.2 190.1 %copy-start = (bf16[7168,32]{0,1:T(8,128)(2,1)S(1)}, bf16[7168,32]{0,1:T(8,128)(2,1)}, u32[]{:S(2)}) copy-start(bf16[7168,32]{0,1:T(8,128)(2,1)} %param.14) | copy-start | bytes 1376260
  7.2 99.3 %all-gather.9.cloned.1.call-start = ((), (), s32[]{:S(2)}) async-start(), calls=%async_computation.2 | async-start | bytes 6881280 | tf_op jit(solution)/shard_map/all_gather | solution.py:111
  106.5 5.4 %copy-start.10 = (bf16[3,128,7168]{2,1,0:T(8,128)(2,1)S(1)}, bf16[3,128,7168]{2,1,0:T(8,128)(2,1)}, u32[]{:S(2)}) copy-start(bf16[3,128,7168]{2,1,0:T(8,128)(2,1)} %all-gather.9.cloned.1.call-done) | copy-start | bytes 16515076
  106.5 6.3 %copy-start.11 = (bf16[1,7168,256]{2,1,0:T(8,128)(2,1)S(1)}, bf16[1,7168,256]{2,1,0:T(8,128)(2,1)}, u32[]{:S(2)}) copy-start(bf16[1,7168,256]{2,1,0:T(8,128)(2,1)} %param.17) | copy-start | bytes 11010052
  112.8 2.0 copy-start.4
  116.5 3.6 copy-start.2
  120.1 62.7 %collective-permute-start = (bf16[3,32,7168]{2,1,0:T(8,128)(2,1)}, bf16[3,32,7168]{2,1,0:T(8,128)(2,1)S(1)}, u32[]{:S(2)}, u32[]{:S(2)}) collective-permute-start(bf16[3,32,7168]{2,1,0:T(8,128)(2,1)} %get-tuple-element.14), channel_id=1, source_target_pairs={{0,32},{32,64},{64,96},{96,0},{1,33},{33,65},{65,97},{97,1},{2,34}... | collective-permute-start | bytes 4128776 | tf_op jit(solution)/shard_map/ppermute | solution.py:46
  121.1 61.6 %collective-permute-start.1 = (bf16[3,32,7168]{2,1,0:T(8,128)(2,1)}, bf16[3,32,7168]{2,1,0:T(8,128)(2,1)S(1)}, u32[]{:S(2)}, u32[]{:S(2)}) collective-permute-start(bf16[3,32,7168]{2,1,0:T(8,128)(2,1)} %get-tuple-element.16), channel_id=1, source_target_pairs={{0,64},{32,96},{64,0},{96,32},{1,65},{33,97},{65,1},{97,33},{2,66}... | collective-permute-start | bytes 4128776 | tf_op jit(solution)/shard_map/ppermute | solution.py:46
  122.6 60.8 %collective-permute-start.2 = (bf16[3,32,7168]{2,1,0:T(8,128)(2,1)}, bf16[3,32,7168]{2,1,0:T(8,128)(2,1)}, u32[]{:S(2)}, u32[]{:S(2)}) collective-permute-start(bf16[3,32,7168]{2,1,0:T(8,128)(2,1)} %get-tuple-element.15), channel_id=1, source_target_pairs={{0,96},{32,0},{64,32},{96,64},{1,97},{33,1},{65,33},{97,65},{2,98}... | collective-permute-start | bytes 4128776 | tf_op jit(solution)/shard_map/ppermute | solution.py:46
  187.3 10.0 %copy-start.5 = (bf16[10,7168]{1,0:T(8,128)(2,1)S(1)}, bf16[10,7168]{1,0:T(8,128)(2,1)}, u32[]{:S(2)}) copy-start(bf16[10,7168]{1,0:T(8,128)(2,1)} %param.12) | copy-start | bytes 430084
  187.3 10.0 %copy-start.6 = (f32[7168]{0:T(1024)S(1)}, f32[7168]{0:T(1024)}, u32[]{:S(2)}) copy-start(f32[7168]{0:T(1024)} %param.13) | copy-start | bytes 86020
  189.8 28.7 %all-to-all-start.1 = ((bf16[32,4,5376]{2,1,0:T(4,128)(2,1)}), bf16[32,4,5376]{2,1,0:T(4,128)(2,1)}, u32[]{:S(2)}, u32[]{:S(2)}) async-start(bf16[32,4,5376]{2,1,0:T(4,128)(2,1)} %reshape.110), calls=%async_computation.1 | async-start | bytes 2752512 | tf_op jit(solution)/shard_map/all_to_all | solution.py:107
  197.2 124.9 %all-gather.11.cloned.1.call-start = ((), (), s32[]{:S(2)}) async-start(), calls=%async_computation.3 | async-start | bytes 29589504 | tf_op jit(solution)/shard_map/all_gather | solution.py:131
  197.7 27.2 %copy-start.7 = (f32[7168]{0:T(1024)S(1)}, f32[7168]{0:T(1024)}, u32[]{:S(2)}) copy-start(f32[7168]{0:T(1024)} %param.19) | copy-start | bytes 86020
  197.8 27.9 %copy-start.3 = (bf16[256,4,512]{2,1,0:T(4,128)(2,1)S(1)}, bf16[256,4,512]{2,1,0:T(4,128)(2,1)}, u32[]{:S(2)}) copy-start(bf16[256,4,512]{2,1,0:T(4,128)(2,1)} %param.21) | copy-start | bytes 3145732
  222.5 3.8 copy-start.9
  224.8 9.1 %copy-start.8 = (s32[256]{0:T(256)S(1)}, s32[256]{0:T(256)}, u32[]{:S(2)}) copy-start(s32[256]{0:T(256)} %param.23) | copy-start | bytes 3076
  395.1 39.7 %copy-start.1 = (bf16[7168,32]{0,1:T(8,128)(2,1)S(1)}, bf16[7168,32]{0,1:T(8,128)(2,1)}, u32[]{:S(2)}) copy-start(bf16[7168,32]{0,1:T(8,128)(2,1)} %param.14) | copy-start | bytes 1376260
Sparse Core Ops, SparseCore 0:
  49.4 57.0 all-gather.8
  225.8 96.2 all-gather.10

commit v7 on v3

--- a/solution.py
+++ b/solution.py
@@ -31,9 +31,7 @@
 
 
 def gathered_sum(values):
-    for axes in gather_groups():
-        values = jnp.sum(lax.all_gather(values, axes, axis=0, tiled=False), axis=0)
-    return values
+    return jnp.sum(lax.all_gather(values, ALL_AXES, axis=0, tiled=False), axis=0)
 
 
 def row_reduce_scatter(parts):

time: 443 us -> 445 us (level)
    all_gather x2 -> x1, blocking collectives: 31.7 us -> 33.6 us  [gathered_sum(): lax.all_gather(values, ALL_AXES, axis=0, tiled=False)]
where the time goes in v7:
time: 445 us; the launch traced here: 443 us
  waiting for transfers between devices  230 us (52%)
  blocking collectives  105 us (24%)
  matrix products  35.7 us (8%)
  other arithmetic  28.4 us (6%)
  local copies, waits for them, and re-layouts  16.7 us (4%)
  between operations  14.6 us (3%)
  starting transfers between devices  12.6 us (3%)
    all_gather x1, waiting for transfers between devices, body(): gathered = lax.all_gather(block, ALL_AXES, axis=0, tiled=True)  88.3 us
    ppermute x3, waiting for transfers between devices, row_reduce_scatter(): total = total + lax.ppermute(chunk, 'row', pairs).astype(jnp.float32)  58.5 us
    all_gather x1, waiting for transfers between devices, body(): shard_piece = lax.all_gather(received, 'row', axis=1, tiled=True)  57 us
    all_gather x2, blocking collectives, merged_stats(): every = lax.all_gather(payload, axes, axis=0, tiled=False)  37.5 us
    all_to_all x1, blocking collectives, body(): lax.all_to_all(send_buffer, VOCAB_AXES, split_axis=1, concat_axis=1, tile...  33.8 us
    all_gather x1, blocking collectives, gathered_sum(): lax.all_gather(values, ALL_AXES, axis=0, tiled=False)  33.6 us
    all_to_all x1, waiting for transfers between devices, body(): lax.all_to_all(summed, VOCAB_AXES, split_axis=1, concat_axis=1, tiled=True)  26.2 us
    dot_general x1, matrix products, body(): lax.dot_general(gathered, head, (((1,), (1,)), ((), ())), preferred_eleme...  22.3 us
  transfers between devices with their start and end apart: 6, of which 5 were waited for; matrix products, arithmetic and copies ran while one was open for 2% of the time, Pallas kernels for 0%

profile of v7, /device:TPU:0, one launch (start us, length us, event | category | flops | bytes accessed | tf_op | source)
XLA Modules:
  0.0 443.1 jit_solution(7040418308892049803)
XLA Ops:
  7.2 0.8 copy.109
  8.0 0.1 fusion.45
  8.2 1.1 fusion.30
  9.3 1.5 fusion
  10.8 1.2 copy.110
  12.0 33.8 %all_to_all.10 = bf16[3,32,7168]{2,0,1:T(4,128)(2,1)S(1)} all-to-all(bf16[3,32,7168]{2,0,1:T(4,128)(2,1)S(1)} %copy.110), channel_id=1, replica_groups=mesh['row'=4,'vz'=4,'vx'=4,'core'=2] {'vz','vx','core'}, dimensions={1} | all-to-all | bytes 2752512 | tf_op jit(solution)/shard_map/all_to_all | solution.py:100
  45.9 1.7 copy.111
  47.6 57.0 %all-gather.7.cloned.1.call-done = bf16[3,128,7168]{2,1,0:T(8,128)(2,1)} async-done(((bf16[3,32,7168]{2,1,0:T(8,128)(2,1)}), bf16[3,128,7168]{2,1,0:T(8,128)(2,1)}) %all-gather.7.cloned.1.call-update) | async-done | bytes 5505040 | tf_op jit(solution)/shard_map/all_gather | solution.py:101
  104.6 5.4 %fusion.5 = f32[384,256]{1,0:T(8,128)S(1)} fusion(bf16[384,7168]{1,0:T(8,128)(2,1)} %bitcast.115, bf16[1,7168,256]{2,1,0:T(8,128)(2,1)} %param.16), kind=kOutput, calls=%fused_computation.12 | convolution fusion | flops 1409286144 | bytes 9568256 | tf_op jit(solution)/shard_map/dot_general | solution.py:103
  110.0 0.9 copy-done.11
  110.9 1.6 fusion.21
  112.5 0.4 copy-done.4
  113.0 1.6 convolution_convert_fusion
  114.6 2.1 dynamic-slice_bitcast_fusion.2
  116.7 1.5 copy-done.2
  118.2 1.0 collective-permute-start
  119.2 1.5 collective-permute-start.1
  120.7 2.3 collective-permute-start.2
  123.1 57.8 %collective-permute-done = bf16[3,32,7168]{2,1,0:T(8,128)(2,1)S(1)} collective-permute-done((bf16[3,32,7168]{2,1,0:T(8,128)(2,1)}, bf16[3,32,7168]{2,1,0:T(8,128)(2,1)S(1)}, u32[]{:S(2)}, u32[]{:S(2)}) %collective-permute-start) | collective-permute-done | bytes 1376288 | tf_op jit(solution)/shard_map/ppermute | solution.py:44
  180.9 0.7 collective-permute-done.2
  181.6 2.6 fusion.9
  184.2 2.4 copy.113
  186.6 7.5 %all-to-all-start.1 = ((bf16[3,32,7168]{2,0,1:T(4,128)(2,1)}), bf16[3,32,7168]{2,0,1:T(4,128)(2,1)}, u32[]{:S(2)}, u32[]{:S(2)}) async-start(bf16[3,32,7168]{2,0,1:T(4,128)(2,1)} %copy.113), calls=%async_computation.1 | async-start | bytes 3670016 | tf_op jit(solution)/shard_map/all_to_all | solution.py:110
  194.1 0.2 all-gather.9.cloned.1.call-start
  194.4 0.4 select_reduce_fusion.1
  194.9 26.2 %all-to-all-done.1 = bf16[3,32,7168]{2,0,1:T(4,128)(2,1)} async-done(((bf16[3,32,7168]{2,0,1:T(4,128)(2,1)}), bf16[3,32,7168]{2,0,1:T(4,128)(2,1)}, u32[]{:S(2)}, u32[]{:S(2)}) %all-to-all-start.1) | async-done | bytes 1376288 | tf_op jit(solution)/shard_map/all_to_all | solution.py:110
  221.1 2.9 multiply_reduce_fusion
  224.0 0.1 multiply_convert_fusion
  224.1 0.7 concatenate.24
  224.9 0.5 reduce_max.45
  225.5 0.1 copy.135
  225.7 0.1 reshape.98
  225.9 7.0 %fusion.11 = (f32[256,4]{1,0:T(8,128)S(1)}, f32[256,4]{1,0:T(8,128)S(1)}) fusion(bf16[256,4,512]{2,1,0:T(4,128)(2,1)S(1)} %copy-done.3, f32[256,4]{1,0:T(8,128)S(1)} %reduce_max.46, s32[256,4]{1,0:T(8,128)S(1)} %copy.135), kind=kLoop, calls=%fused_computation.22 | loop fusion | flops 3143680 | bytes 1064960 | tf_op jit(solution)/shard_map/reduce_sum | solution.py:80
  233.0 0.1 copy.122
  233.1 0.1 fusion.42
  233.2 88.3 %all-gather.9.cloned.1.call-done = bf16[2048,7168]{1,0:T(8,128)(2,1)} async-done(((bf16[16,7168]{1,0:T(8,128)(2,1)}), bf16[2048,7168]{1,0:T(8,128)(2,1)}) %all-gather.9.cloned.1.call-update) | async-done | bytes 29360144 | tf_op jit(solution)/shard_map/all_gather | solution.py:121
  321.5 22.3 %fusion.59 = (f32[2048]{0:T(1024)S(1)}, f32[2048,512]{1,0:T(8,128)}) fusion(bf16[2048,7168]{1,0:T(8,128)(2,1)} %all-gather.9.cloned.1.call-done, bf16[512,7168]{1,0:T(8,128)(2,1)} %param.20), kind=kOutput, calls=%fused_computation.102 | convolution fusion | flops 15033432064 | bytes 40902656 | tf_op jit(solution)/shard_map/dot_general | solution.py:123
  343.9 3.2 exponential_reduce_fusion
  347.2 0.1 reshape.97
  347.3 0.1 reshape.96
  347.5 0.1 reduce_sum.155
  347.6 0.1 reshape.99
  347.8 24.3 %all-gather = f32[48,256,9]{1,2,0:T(8,128)S(1)} all-gather(f32[3,256,9]{1,2,0:T(8,128)S(1)} %pad_maximum_fusion.1), channel_id=2, replica_groups=mesh['row'=4,'vz'=4,'vx'=4,'core'=2] {'row','vz'}, dimensions={0}, use_global_device_ids=true | all-gather | bytes 470016 | tf_op jit(solution)/shard_map/all_gather | solution.py:26
  372.3 13.3 %all-gather.1 = f32[24,256,9]{1,2,0:T(8,128)S(1)} all-gather(f32[3,256,9]{1,2,0:T(8,128)S(1)} %copy.124), channel_id=3, replica_groups=mesh['row'=4,'vz'=4,'vx'=4,'core'=2] {'vx','core'}, dimensions={0}, use_global_device_ids=true | all-gather | bytes 248832 | tf_op jit(solution)/shard_map/all_gather | solution.py:26
  385.6 0.4 copy.133
  386.1 1.4 copy.132
  387.4 0.1 copy.137
  387.6 0.1 copy.138
  387.7 1.4 fusion.29
  389.2 0.1 slice_divide_fusion
  389.3 0.1 reshape.100
  389.5 2.6 exponential_multiply_fusion
  392.1 1.5 slice_reduce_fusion.1
  393.6 0.2 stack.41
  393.8 0.2 stack.42
  394.0 0.5 pad_maximum_fusion
  394.4 0.4 reshape.103
  394.8 0.1 fusion.41
  395.0 5.6 %fusion.16 = f32[256,512]{1,0:T(8,128)S(1)} fusion(bf16[256,4,512]{2,1,0:T(4,128)(2,1)S(1)} %copy-done.3, f32[256,4]{1,0:T(8,128)S(1)} %get-tuple-element.24, f32[256,4]{1,0:T(8,128)S(1)} %get-tuple-element.23, f32[256,4]{1,0:T(8,128)S(1)} %bitcast.108), kind=kLoop, calls=%fused_computation.30 | loop fusion | flops 2490368 | bytes 1585152 | tf_op jit(solution)/shard_map/reduce_sum | solution.py:175
  400.6 0.1 fusion.37
  400.7 33.6 %all-gather.3 = f32[128,1,256]{2,1,0:T(1,128)S(1)} all-gather(f32[1,1,256]{2,1,0:T(1,128)S(1)} %bitcast.114), channel_id=4, replica_groups=mesh['row'=4,'vz'=4,'vx'=4,'core'=2] {'row','vz','vx','core'}, dimensions={0}, use_global_device_ids=true | all-gather | bytes 132096 | tf_op jit(solution)/shard_map/all_gather | solution.py:34
  434.4 0.2 reduce_sum.164
  434.5 1.0 divide_sqrt_fusion
  435.6 0.7 copy.129
  (60 shorter events, 1.3 us)
Async XLA Ops:
  7.2 187.2 %copy-start = (bf16[7168,32]{0,1:T(8,128)(2,1)S(1)}, bf16[7168,32]{0,1:T(8,128)(2,1)}, u32[]{:S(2)}) copy-start(bf16[7168,32]{0,1:T(8,128)(2,1)} %param.14) | copy-start | bytes 1376260
  7.2 97.4 %all-gather.7.cloned.1.call-start = ((), (), s32[]{:S(2)}) async-start(), calls=%async_computation.2 | async-start | bytes 6881280 | tf_op jit(solution)/shard_map/all_gather | solution.py:101
  104.6 5.4 %copy-start.10 = (bf16[3,128,7168]{2,1,0:T(8,128)(2,1)S(1)}, bf16[3,128,7168]{2,1,0:T(8,128)(2,1)}, u32[]{:S(2)}) copy-start(bf16[3,128,7168]{2,1,0:T(8,128)(2,1)} %all-gather.7.cloned.1.call-done) | copy-start | bytes 16515076
  104.6 6.3 %copy-start.11 = (bf16[1,7168,256]{2,1,0:T(8,128)(2,1)S(1)}, bf16[1,7168,256]{2,1,0:T(8,128)(2,1)}, u32[]{:S(2)}) copy-start(bf16[1,7168,256]{2,1,0:T(8,128)(2,1)} %param.17) | copy-start | bytes 11010052
  110.9 2.0 copy-start.4
  114.6 3.6 copy-start.2
  118.2 62.7 %collective-permute-start = (bf16[3,32,7168]{2,1,0:T(8,128)(2,1)}, bf16[3,32,7168]{2,1,0:T(8,128)(2,1)S(1)}, u32[]{:S(2)}, u32[]{:S(2)}) collective-permute-start(bf16[3,32,7168]{2,1,0:T(8,128)(2,1)} %get-tuple-element.16), channel_id=1, source_target_pairs={{0,32},{32,64},{64,96},{96,0},{1,33},{33,65},{65,97},{97,1},{2,34}... | collective-permute-start | bytes 4128776 | tf_op jit(solution)/shard_map/ppermute | solution.py:44
  119.2 61.6 %collective-permute-start.1 = (bf16[3,32,7168]{2,1,0:T(8,128)(2,1)}, bf16[3,32,7168]{2,1,0:T(8,128)(2,1)S(1)}, u32[]{:S(2)}, u32[]{:S(2)}) collective-permute-start(bf16[3,32,7168]{2,1,0:T(8,128)(2,1)} %get-tuple-element.18), channel_id=1, source_target_pairs={{0,64},{32,96},{64,0},{96,32},{1,65},{33,97},{65,1},{97,33},{2,66}... | collective-permute-start | bytes 4128776 | tf_op jit(solution)/shard_map/ppermute | solution.py:44
  120.7 60.8 %collective-permute-start.2 = (bf16[3,32,7168]{2,1,0:T(8,128)(2,1)}, bf16[3,32,7168]{2,1,0:T(8,128)(2,1)}, u32[]{:S(2)}, u32[]{:S(2)}) collective-permute-start(bf16[3,32,7168]{2,1,0:T(8,128)(2,1)} %get-tuple-element.17), channel_id=1, source_target_pairs={{0,96},{32,0},{64,32},{96,64},{1,97},{33,1},{65,33},{97,65},{2,98}... | collective-permute-start | bytes 4128776 | tf_op jit(solution)/shard_map/ppermute | solution.py:44
  184.2 10.2 %copy-start.5 = (bf16[10,7168]{1,0:T(8,128)(2,1)S(1)}, bf16[10,7168]{1,0:T(8,128)(2,1)}, u32[]{:S(2)}) copy-start(bf16[10,7168]{1,0:T(8,128)(2,1)} %param.12) | copy-start | bytes 430084
  184.2 10.2 %copy-start.6 = (f32[7168]{0:T(1024)S(1)}, f32[7168]{0:T(1024)}, u32[]{:S(2)}) copy-start(f32[7168]{0:T(1024)} %param.13) | copy-start | bytes 86020
  186.6 37.4 %copy-start.7 = (f32[7168]{0:T(1024)S(1)}, f32[7168]{0:T(1024)}, u32[]{:S(2)}) copy-start(f32[7168]{0:T(1024)} %param.19) | copy-start | bytes 86020
  186.6 34.5 %all-to-all-start.1 = ((bf16[3,32,7168]{2,0,1:T(4,128)(2,1)}), bf16[3,32,7168]{2,0,1:T(4,128)(2,1)}, u32[]{:S(2)}, u32[]{:S(2)}) async-start(bf16[3,32,7168]{2,0,1:T(4,128)(2,1)} %copy.113), calls=%async_computation.1 | async-start | bytes 3670016 | tf_op jit(solution)/shard_map/all_to_all | solution.py:110
  194.1 30.8 %copy-start.3 = (bf16[256,4,512]{2,1,0:T(4,128)(2,1)S(1)}, bf16[256,4,512]{2,1,0:T(4,128)(2,1)}, u32[]{:S(2)}) copy-start(bf16[256,4,512]{2,1,0:T(4,128)(2,1)} %param.21) | copy-start | bytes 3145732
  194.1 31.4 %copy-start.9 = (s32[256,4]{0,1:T(4,128)S(1)}, s32[256,4]{0,1:T(4,128)}, u32[]{:S(2)}) copy-start(s32[256,4]{0,1:T(4,128)} %param.22) | copy-start | bytes 12292
  194.1 127.4 %all-gather.9.cloned.1.call-start = ((), (), s32[]{:S(2)}) async-start(), calls=%async_computation.3 | async-start | bytes 29589504 | tf_op jit(solution)/shard_map/all_gather | solution.py:121
  224.0 9.1 %copy-start.8 = (s32[256]{0:T(256)S(1)}, s32[256]{0:T(256)}, u32[]{:S(2)}) copy-start(s32[256]{0:T(256)} %param.23) | copy-start | bytes 3076
  394.8 41.4 %copy-start.1 = (bf16[7168,32]{0,1:T(8,128)(2,1)S(1)}, bf16[7168,32]{0,1:T(8,128)(2,1)}, u32[]{:S(2)}) copy-start(bf16[7168,32]{0,1:T(8,128)(2,1)} %param.14) | copy-start | bytes 1376260
Sparse Core Ops, SparseCore 0:
  47.7 56.8 all-gather.6
  225.0 96.4 all-gather.8

commit v8 on v3

--- a/solution.py
+++ b/solution.py
@@ -17,7 +17,7 @@
 
 
 def gather_groups():
-    return (("row", "vz"), ("vx", "core"))
+    return (("vx", "core"), ("row", "vz"))
 
 
 def merged_stats(top, total, pick):

time: 443 us -> 443 us (level)
  no operation moved by 1% of the time
where the time goes in v8:
time: 443 us; the launch traced here: 442 us
  waiting for transfers between devices  229 us (52%)
  blocking collectives  103 us (23%)
  matrix products  36.2 us (8%)
  other arithmetic  28.9 us (7%)
  local copies, waits for them, and re-layouts  17.7 us (4%)
  between operations  14.6 us (3%)
  starting transfers between devices  12.5 us (3%)
    all_gather x1, waiting for transfers between devices, body(): gathered = lax.all_gather(block, ALL_AXES, axis=0, tiled=True)  88.3 us
    ppermute x3, waiting for transfers between devices, row_reduce_scatter(): total = total + lax.ppermute(chunk, 'row', pairs).astype(jnp.float32)  58.5 us
    all_gather x1, waiting for transfers between devices, body(): shard_piece = lax.all_gather(received, 'row', axis=1, tiled=True)  57 us
    all_gather x2, blocking collectives, merged_stats(): every = lax.all_gather(payload, axes, axis=0, tiled=False)  37.6 us
    all_to_all x1, blocking collectives, body(): lax.all_to_all(send_buffer, VOCAB_AXES, split_axis=1, concat_axis=1, tile...  33.8 us
    all_gather x2, blocking collectives, gathered_sum(): values = jnp.sum(lax.all_gather(values, axes, axis=0, tiled=False), axis=0)  31.8 us
    all_to_all x1, waiting for transfers between devices, body(): lax.all_to_all(summed, VOCAB_AXES, split_axis=1, concat_axis=1, tiled=True)  25.2 us
    dot_general x1, matrix products, body(): lax.dot_general(gathered, head, (((1,), (1,)), ((), ())), preferred_eleme...  22.3 us
  transfers between devices with their start and end apart: 6, of which 5 were waited for; matrix products, arithmetic and copies ran while one was open for 2% of the time, Pallas kernels for 0%

profile of v8, /device:TPU:0, one launch (start us, length us, event | category | flops | bytes accessed | tf_op | source)
XLA Modules:
  0.0 442.0 jit_solution(3679573531947173073)
XLA Ops:
  7.2 0.8 copy.109
  8.0 0.1 fusion.45
  8.2 1.1 fusion.30
  9.3 1.5 fusion
  10.8 1.2 copy.110
  12.0 33.8 %all_to_all.10 = bf16[3,32,7168]{2,0,1:T(4,128)(2,1)S(1)} all-to-all(bf16[3,32,7168]{2,0,1:T(4,128)(2,1)S(1)} %copy.110), channel_id=1, replica_groups=mesh['row'=4,'vz'=4,'vx'=4,'core'=2] {'vz','vx','core'}, dimensions={1} | all-to-all | bytes 2752512 | tf_op jit(solution)/shard_map/all_to_all | solution.py:102
  45.9 1.7 copy.111
  47.6 57.0 %all-gather.9.cloned.1.call-done = bf16[3,128,7168]{2,1,0:T(8,128)(2,1)} async-done(((bf16[3,32,7168]{2,1,0:T(8,128)(2,1)}), bf16[3,128,7168]{2,1,0:T(8,128)(2,1)}) %all-gather.9.cloned.1.call-update) | async-done | bytes 5505040 | tf_op jit(solution)/shard_map/all_gather | solution.py:103
  104.6 5.4 %fusion.5 = f32[384,256]{1,0:T(8,128)S(1)} fusion(bf16[384,7168]{1,0:T(8,128)(2,1)} %bitcast.117, bf16[1,7168,256]{2,1,0:T(8,128)(2,1)} %param.16), kind=kOutput, calls=%fused_computation.12 | convolution fusion | flops 1409286144 | bytes 9568256 | tf_op jit(solution)/shard_map/dot_general | solution.py:105
  110.0 0.9 copy-done.11
  110.9 1.6 fusion.24
  112.5 0.4 copy-done.5
  113.0 1.6 convolution_convert_fusion
  114.6 2.1 dynamic-slice_bitcast_fusion.2
  116.7 1.5 copy-done.2
  118.2 1.0 collective-permute-start
  119.2 1.5 collective-permute-start.1
  120.7 2.3 collective-permute-start.2
  123.1 57.8 %collective-permute-done = bf16[3,32,7168]{2,1,0:T(8,128)(2,1)S(1)} collective-permute-done((bf16[3,32,7168]{2,1,0:T(8,128)(2,1)}, bf16[3,32,7168]{2,1,0:T(8,128)(2,1)S(1)}, u32[]{:S(2)}, u32[]{:S(2)}) %collective-permute-start) | collective-permute-done | bytes 1376288 | tf_op jit(solution)/shard_map/ppermute | solution.py:46
  180.9 0.7 collective-permute-done.2
  181.6 2.6 fusion.9
  184.2 2.4 copy.113
  186.6 7.4 %all-to-all-start.1 = ((bf16[3,32,7168]{2,0,1:T(4,128)(2,1)}), bf16[3,32,7168]{2,0,1:T(4,128)(2,1)S(1)}, u32[]{:S(2)}, u32[]{:S(2)}) async-start(bf16[3,32,7168]{2,0,1:T(4,128)(2,1)} %copy.113), calls=%async_computation.1 | async-start | bytes 3670016 | tf_op jit(solution)/shard_map/all_to_all | solution.py:112
  194.0 0.2 all-gather.11.cloned.1.call-start
  194.3 1.4 select_reduce_fusion.1
  195.8 25.2 %all-to-all-done.1 = bf16[3,32,7168]{2,0,1:T(4,128)(2,1)S(1)} async-done(((bf16[3,32,7168]{2,0,1:T(4,128)(2,1)}), bf16[3,32,7168]{2,0,1:T(4,128)(2,1)S(1)}, u32[]{:S(2)}, u32[]{:S(2)}) %all-to-all-start.1) | async-done | bytes 1376288 | tf_op jit(solution)/shard_map/all_to_all | solution.py:112
  221.0 2.3 multiply_reduce_fusion
  223.4 0.1 multiply_convert_fusion
  223.5 0.7 concatenate.24
  224.2 0.5 reduce_max.45
  224.8 0.1 copy.135
  225.0 0.1 reshape.98
  225.2 7.0 %fusion.11 = (f32[256,4]{1,0:T(8,128)S(1)}, f32[256,4]{1,0:T(8,128)S(1)}) fusion(bf16[256,4,512]{2,1,0:T(4,128)(2,1)S(1)} %copy-done.3, f32[256,4]{1,0:T(8,128)S(1)} %reduce_max.46, s32[256,4]{1,0:T(8,128)S(1)} %copy.135), kind=kLoop, calls=%fused_computation.22 | loop fusion | flops 3143680 | bytes 1064960 | tf_op jit(solution)/shard_map/reduce_sum | solution.py:82
  232.3 0.1 copy.122
  232.4 0.1 fusion.42
  232.5 88.3 %all-gather.11.cloned.1.call-done = bf16[2048,7168]{1,0:T(8,128)(2,1)} async-done(((bf16[16,7168]{1,0:T(8,128)(2,1)}), bf16[2048,7168]{1,0:T(8,128)(2,1)}) %all-gather.11.cloned.1.call-update) | async-done | bytes 29360144 | tf_op jit(solution)/shard_map/all_gather | solution.py:123
  320.8 22.3 %fusion.59 = (f32[2048]{0:T(1024)S(1)}, f32[2048,512]{1,0:T(8,128)}) fusion(bf16[2048,7168]{1,0:T(8,128)(2,1)} %all-gather.11.cloned.1.call-done, bf16[512,7168]{1,0:T(8,128)(2,1)} %param.20), kind=kOutput, calls=%fused_computation.102 | convolution fusion | flops 15033432064 | bytes 40902656 | tf_op jit(solution)/shard_map/dot_general | solution.py:125
  343.3 3.2 exponential_reduce_fusion
  346.5 0.1 reshape.97
  346.7 0.1 reshape.96
  346.9 0.1 reduce_sum.164
  347.0 0.1 reshape.99
  347.2 13.3 %all-gather = f32[24,256,9]{1,2,0:T(8,128)S(1)} all-gather(f32[3,256,9]{1,2,0:T(8,128)S(1)} %pad_maximum_fusion.1), channel_id=2, replica_groups=mesh['row'=4,'vz'=4,'vx'=4,'core'=2] {'vx','core'}, dimensions={0}, use_global_device_ids=true | all-gather | bytes 248832 | tf_op jit(solution)/shard_map/all_gather | solution.py:26
  360.6 24.3 %all-gather.1 = f32[48,256,9]{1,2,0:T(8,128)S(1)} all-gather(f32[3,256,9]{1,2,0:T(8,128)S(1)} %copy.124), channel_id=3, replica_groups=mesh['row'=4,'vz'=4,'vx'=4,'core'=2] {'row','vz'}, dimensions={0}, use_global_device_ids=true | all-gather | bytes 470016 | tf_op jit(solution)/shard_map/all_gather | solution.py:26
  385.0 0.6 copy.133
  385.6 0.1 bitcast_reduce_fusion
  385.8 2.0 copy.132
  387.8 0.1 copy.137
  387.9 0.1 copy.138
  388.1 2.0 fusion.18
  390.1 0.1 slice_divide_fusion
  390.4 2.6 exponential_multiply_fusion
  393.0 1.5 slice_reduce_fusion.1
  394.5 0.2 stack.41
  394.7 0.2 stack.42
  394.9 0.5 pad_maximum_fusion
  395.4 0.4 reshape.103
  395.7 0.1 fusion.38
  395.9 5.6 %fusion.19 = f32[256,512]{1,0:T(8,128)S(1)} fusion(bf16[256,4,512]{2,1,0:T(4,128)(2,1)S(1)} %copy-done.4, f32[256,4]{1,0:T(8,128)S(1)} %get-tuple-element.24, f32[256,4]{1,0:T(8,128)S(1)} %get-tuple-element.23, f32[256,4]{1,0:T(8,128)S(1)} %bitcast.109), kind=kLoop, calls=%fused_computation.35 | loop fusion | flops 2490368 | bytes 1585152 | tf_op jit(solution)/shard_map/reduce_sum | solution.py:177
  401.5 0.1 fusion.34
  401.7 10.2 %all-gather.4 = f32[8,1,256]{2,1,0:T(1,128)S(1)} all-gather(f32[1,1,256]{2,1,0:T(1,128)S(1)} %bitcast.115), channel_id=4, replica_groups=mesh['row'=4,'vz'=4,'vx'=4,'core'=2] {'vx','core'}, dimensions={0}, use_global_device_ids=true | all-gather | bytes 9216 | tf_op jit(solution)/shard_map/all_gather | solution.py:35
  411.9 21.6 %all-gather.5 = f32[16,1,256]{2,1,0:T(1,128)S(1)} all-gather(f32[1,1,256]{2,1,0:T(1,128)S(1)} %bitcast.116), channel_id=5, replica_groups=mesh['row'=4,'vz'=4,'vx'=4,'core'=2] {'row','vz'}, dimensions={0}, use_global_device_ids=true | all-gather | bytes 17408 | tf_op jit(solution)/shard_map/all_gather | solution.py:35
  433.5 1.0 divide_sqrt_fusion
  434.5 0.7 copy.129
  (62 shorter events, 1.4 us)
Async XLA Ops:
  7.2 187.1 %copy-start = (bf16[7168,32]{0,1:T(8,128)(2,1)S(1)}, bf16[7168,32]{0,1:T(8,128)(2,1)}, u32[]{:S(2)}) copy-start(bf16[7168,32]{0,1:T(8,128)(2,1)} %param.14) | copy-start | bytes 1376260
  7.2 97.4 %all-gather.9.cloned.1.call-start = ((), (), s32[]{:S(2)}) async-start(), calls=%async_computation.2 | async-start | bytes 6881280 | tf_op jit(solution)/shard_map/all_gather | solution.py:103
  104.6 5.4 %copy-start.10 = (bf16[3,128,7168]{2,1,0:T(8,128)(2,1)S(1)}, bf16[3,128,7168]{2,1,0:T(8,128)(2,1)}, u32[]{:S(2)}) copy-start(bf16[3,128,7168]{2,1,0:T(8,128)(2,1)} %all-gather.9.cloned.1.call-done) | copy-start | bytes 16515076
  104.6 6.3 %copy-start.11 = (bf16[1,7168,256]{2,1,0:T(8,128)(2,1)S(1)}, bf16[1,7168,256]{2,1,0:T(8,128)(2,1)}, u32[]{:S(2)}) copy-start(bf16[1,7168,256]{2,1,0:T(8,128)(2,1)} %param.17) | copy-start | bytes 11010052
  110.9 2.0 copy-start.5
  114.6 3.6 copy-start.2
  118.2 62.7 %collective-permute-start = (bf16[3,32,7168]{2,1,0:T(8,128)(2,1)}, bf16[3,32,7168]{2,1,0:T(8,128)(2,1)S(1)}, u32[]{:S(2)}, u32[]{:S(2)}) collective-permute-start(bf16[3,32,7168]{2,1,0:T(8,128)(2,1)} %get-tuple-element.16), channel_id=1, source_target_pairs={{0,32},{32,64},{64,96},{96,0},{1,33},{33,65},{65,97},{97,1},{2,34}... | collective-permute-start | bytes 4128776 | tf_op jit(solution)/shard_map/ppermute | solution.py:46
  119.2 61.6 %collective-permute-start.1 = (bf16[3,32,7168]{2,1,0:T(8,128)(2,1)}, bf16[3,32,7168]{2,1,0:T(8,128)(2,1)S(1)}, u32[]{:S(2)}, u32[]{:S(2)}) collective-permute-start(bf16[3,32,7168]{2,1,0:T(8,128)(2,1)} %get-tuple-element.18), channel_id=1, source_target_pairs={{0,64},{32,96},{64,0},{96,32},{1,65},{33,97},{65,1},{97,33},{2,66}... | collective-permute-start | bytes 4128776 | tf_op jit(solution)/shard_map/ppermute | solution.py:46
  120.7 60.8 %collective-permute-start.2 = (bf16[3,32,7168]{2,1,0:T(8,128)(2,1)}, bf16[3,32,7168]{2,1,0:T(8,128)(2,1)}, u32[]{:S(2)}, u32[]{:S(2)}) collective-permute-start(bf16[3,32,7168]{2,1,0:T(8,128)(2,1)} %get-tuple-element.17), channel_id=1, source_target_pairs={{0,96},{32,0},{64,32},{96,64},{1,97},{33,1},{65,33},{97,65},{2,98}... | collective-permute-start | bytes 4128776 | tf_op jit(solution)/shard_map/ppermute | solution.py:46
  184.2 10.1 %copy-start.6 = (f32[7168]{0:T(1024)S(1)}, f32[7168]{0:T(1024)}, u32[]{:S(2)}) copy-start(f32[7168]{0:T(1024)} %param.13) | copy-start | bytes 86020
  186.6 36.7 %copy-start.7 = (f32[7168]{0:T(1024)S(1)}, f32[7168]{0:T(1024)}, u32[]{:S(2)}) copy-start(f32[7168]{0:T(1024)} %param.19) | copy-start | bytes 86020
  186.6 34.4 %all-to-all-start.1 = ((bf16[3,32,7168]{2,0,1:T(4,128)(2,1)}), bf16[3,32,7168]{2,0,1:T(4,128)(2,1)S(1)}, u32[]{:S(2)}, u32[]{:S(2)}) async-start(bf16[3,32,7168]{2,0,1:T(4,128)(2,1)} %copy.113), calls=%async_computation.1 | async-start | bytes 3670016 | tf_op jit(solution)/shard_map/all_to_all | solution.py:112
  194.0 30.2 %copy-start.3 = (bf16[256,4,512]{2,1,0:T(4,128)(2,1)S(1)}, bf16[256,4,512]{2,1,0:T(4,128)(2,1)}, u32[]{:S(2)}) copy-start(bf16[256,4,512]{2,1,0:T(4,128)(2,1)} %param.21) | copy-start | bytes 3145732
  194.0 30.8 %copy-start.9 = (s32[256,4]{0,1:T(4,128)S(1)}, s32[256,4]{0,1:T(4,128)}, u32[]{:S(2)}) copy-start(s32[256,4]{0,1:T(4,128)} %param.22) | copy-start | bytes 12292
  194.0 126.8 %all-gather.11.cloned.1.call-start = ((), (), s32[]{:S(2)}) async-start(), calls=%async_computation.3 | async-start | bytes 29589504 | tf_op jit(solution)/shard_map/all_gather | solution.py:123
  223.3 9.1 %copy-start.8 = (s32[256]{0:T(256)S(1)}, s32[256]{0:T(256)}, u32[]{:S(2)}) copy-start(s32[256]{0:T(256)} %param.23) | copy-start | bytes 3076
  394.5 1.4 copy-start.4
  395.4 39.8 %copy-start.1 = (bf16[7168,32]{0,1:T(8,128)(2,1)S(1)}, bf16[7168,32]{0,1:T(8,128)(2,1)}, u32[]{:S(2)}) copy-start(bf16[7168,32]{0,1:T(8,128)(2,1)} %param.14) | copy-start | bytes 1376260
Sparse Core Ops, SparseCore 0:
  47.7 56.8 all-gather.8
  224.3 96.4 all-gather.10
